TPU v7x, 512 devices: a whole 4x8x8 slice. The times are simulated.
512 devices in a mesh: slab: 64 (over z, x, core), obs: 8 (over y).
Axes of the slice: x: 4, y: 8, z: 8, core: 2. Of those that a mesh axis runs over, the one named last changes fastest.
Arguments:
- background_members: float32 [64, 1048576], P('slab', 'obs'), may hold values from -6 to 6
- measurement_jitter: bfloat16 [64, 8, 65536], P(None, 'obs', 'slab'), may hold values from -5 to 5
- measurement_readings: float32 [8, 65536], P('obs', 'slab'), may hold values from -8 to 8
- measurement_noise_spread: float32 [8, 65536], P('obs', 'slab'), may hold values from 0.2 to 2
- measurement_grid_location: int32 [8, 65536], P('obs', 'slab'), may hold values from 0 to 2047
- active_tallies: int32 [8, 64], P('obs', 'slab'), may hold values from 128 to 1024, as said below
- coupling_listing: int32 [8, 2048, 8], P('obs', 'slab'), may hold values from 0 to 63, as said below
- taper_factors: float32 [8, 2048, 8], P('obs', 'slab'), may hold values from 0.1 to 1
Outputs:
- analysis: float32 [64, 1048576], P('slab', 'obs')
Inputs may be any that keep to these rules, and one draw needn't show every extreme that they name: `active_tallies`: some region of some group holds 1024 live observations; slots beyond a region's count are padding. `coupling_listing`: the 8 observation blocks listed for a state block are distinct.
All inputs are finite; a program needn't handle non-finite values.
Results may differ from a plain program's by a relative error of at most 0.0063.
Values may be sent and summed in bfloat16 or wider, within the bound.
No kernel may reach another device: no remote copies, remote signals or barrier semaphores. Data moves between devices by JAX's collectives and lax.ppermute only.
A program may use at most 64 MiB of HBM per device.

v0:
```python
import math

import jax
import jax.numpy as jnp
from jax import lax
from jax.sharding import PartitionSpec as P

OB = 128


highest = lax.Precision.HIGHEST


def compute_increment(
    tile_work,
    measurement_jitter,
    measurement_readings,
    measurement_noise_spread,
    measurement_grid_location,
    active_tallies,
    coupling_listing,
    taper_factors,
):
    members = tile_work.shape[0]
    points = tile_work.shape[1]
    blocks = coupling_listing.shape[1]
    block_width = points // blocks
    deviation = tile_work - jnp.mean(tile_work, axis=0, keepdims=True)
    positions = measurement_grid_location[0]
    obs_count = positions.shape[0]
    prior_value = jnp.take(tile_work, positions, axis=1)
    prior_shift = prior_value - jnp.mean(prior_value, axis=0, keepdims=True)
    spread = jnp.sum(prior_shift * prior_shift, axis=0, keepdims=True) / (members - 1)
    usable = jnp.arange(obs_count, dtype=jnp.int32)[None, :] < active_tallies[0, 0]
    innovation = (
        measurement_readings + measurement_jitter[:, 0, :].astype(jnp.float32) - prior_value
    ) / (spread + measurement_noise_spread)
    gain_input = jnp.where(usable, innovation, jnp.float32(0.0)).astype(jnp.bfloat16)
    prior_low = prior_shift.astype(jnp.bfloat16)
    block_links = coupling_listing[0]
    factor = taper_factors[0] / (members - 1)
    gathered = (
        lax.all_gather(prior_low, "obs", axis=1, tiled=True),
        lax.all_gather(gain_input, "obs", axis=1, tiled=True),
    )
    all_prior = gathered[0].reshape(members, -1, OB)
    all_gain = gathered[1].reshape(members, -1, OB)
    group_size = math.gcd(blocks, 8)
    group_count = blocks // group_size

    def one_group(group_index, running):
        first_block = group_index * group_size
        local_dev = lax.dynamic_slice_in_dim(
            deviation, first_block * block_width, group_size * block_width, 1
        )
        local_dev = local_dev.reshape(members, group_size, block_width)
        chosen = lax.dynamic_slice_in_dim(block_links, first_block, group_size, 0)
        scales = lax.dynamic_slice_in_dim(factor, first_block, group_size, 0)
        picked_prior = jnp.take(all_prior, chosen, axis=1).astype(jnp.float32)
        picked_gain = jnp.take(all_gain, chosen, axis=1).astype(jnp.float32)
        covariance = jnp.einsum("mgp,mglo->glpo", local_dev, picked_prior, precision=highest)
        update = jnp.einsum("glpo,mglo,gl->mgp", covariance, picked_gain, scales, precision=highest)
        update = update.reshape(members, group_size * block_width)
        return lax.dynamic_update_slice_in_dim(running, update, first_block * block_width, 1)

    increment = lax.fori_loop(0, group_count, one_group, jnp.zeros_like(deviation))
    return increment.astype(jnp.bfloat16)


def local(
    background_members,
    measurement_jitter,
    measurement_readings,
    measurement_noise_spread,
    measurement_grid_location,
    active_tallies,
    coupling_listing,
    taper_factors,
):
    grid_segment_piece = lax.all_to_all(
        background_members, "slab", split_axis=1, concat_axis=0, tiled=True
    )
    tile_work = lax.optimization_barrier(grid_segment_piece.astype(jnp.bfloat16)).astype(
        jnp.float32
    )
    reduced_correction = compute_increment(
        tile_work,
        measurement_jitter,
        measurement_readings,
        measurement_noise_spread,
        measurement_grid_location,
        active_tallies,
        coupling_listing,
        taper_factors,
    )
    analysis = grid_segment_piece + lax.optimization_barrier(reduced_correction).astype(jnp.float32)
    return lax.all_to_all(analysis, "slab", split_axis=0, concat_axis=1, tiled=True)


def solution(mesh):
    return jax.shard_map(
        local,
        mesh=mesh,
        in_specs=(
            P("slab", "obs"),
            P(None, "obs", "slab"),
            P("obs", "slab"),
            P("obs", "slab"),
            P("obs", "slab"),
            P("obs", "slab"),
            P("obs", "slab", None),
            P("obs", "slab", None),
        ),
        out_specs=P("slab", "obs"),
        check_vma=False,
    )
```

profile of v0, /device:TPU:1, one launch (start us, length us, event | category | flops | bytes accessed | tf_op | source)
XLA Modules:
  0.0 229.1 jit_solution(7997305621396136883)
XLA Ops:
  6.5 14.8 %all-to-all-start = ((f32[1,64,2048]{2,0,1:T(1,128)}), f32[1,64,2048]{2,0,1:T(1,128)S(1)}, u32[]{:S(2)}, u32[]{:S(2)}) async-start(f32[1,64,2048]{2,0,1:T(1,128)} %bitcast.93), calls=%async_computation | async-start | bytes 1048576 | tf_op jit(solution)/shard_map/all_to_all | solution.py:80
  22.1 1.1 copy.33
  23.1 0.7 iota_compare_fusion
  23.8 0.7 compare_select_fusion.1
  24.5 14.5 %all-to-all-done = f32[1,64,2048]{2,0,1:T(1,128)S(1)} async-done(((f32[1,64,2048]{2,0,1:T(1,128)}), f32[1,64,2048]{2,0,1:T(1,128)S(1)}, u32[]{:S(2)}, u32[]{:S(2)}) %all-to-all-start) | async-done | bytes 524320 | tf_op jit(solution)/shard_map/all_to_all | solution.py:80
  39.1 0.2 copy.51
  39.2 0.7 copy-done
  39.9 0.2 copy.34
  40.1 2.8 %gather_fusion.2 = f32[1024,64]{1,0:T(8,128)S(1)} fusion(f32[64,2048]{0,1:T(8,128)S(1)} %copy.34, s32[1024]{0:T(1024)S(1)} %broadcast_clamp_fusion), kind=kCustom, calls=%fused_computation.2 | custom fusion | bytes 528384 | tf_op jit(solution)/shard_map/jit(_take)/gather | solution.py:31
  43.0 0.4 select_reduce_fusion
  43.3 1.0 fusion.18
  44.4 1.6 fusion.17
  46.1 0.7 all-gather.5.cloned.1.call-update
  46.8 0.1 copy.32
  47.0 0.8 broadcast_subtract_fusion
  47.8 33.9 %all-gather.3.cloned.1.call-done = bf16[64,8192]{0,1:T(8,128)(2,1)} async-done(((bf16[64,1024]{0,1:T(8,128)(2,1)}), bf16[64,8192]{0,1:T(8,128)(2,1)}) %all-gather.3.cloned.1.call-update) | async-done | bytes 1048592 | tf_op jit(solution)/shard_map/all_gather | solution.py:44
  81.8 2.7 %copy.35 = bf16[64,64,128]{2,0,1:T(8,128)(2,1)} copy(bf16[64,64,128]{0,2,1:T(8,128)(2,1)} %bitcast.90) | data formatting | bytes 2097152 | tf_op jit(solution)/shard_map/while | solution.py:66
  84.4 41.5 %all-gather.5.cloned.1.call-done = bf16[64,8192]{0,1:T(8,128)(2,1)} async-done(((bf16[64,1024]{0,1:T(8,128)(2,1)}), bf16[64,8192]{0,1:T(8,128)(2,1)}) %all-gather.5.cloned.1.call-update) | async-done | bytes 1048592 | tf_op jit(solution)/shard_map/all_gather | solution.py:43
  126.0 2.7 %copy.36 = bf16[64,64,128]{2,0,1:T(8,128)(2,1)} copy(bf16[64,64,128]{0,2,1:T(8,128)(2,1)} %bitcast.91) | data formatting | bytes 2097152 | tf_op jit(solution)/shard_map/while | solution.py:66
  128.7 58.3 %while.15 = (s32[]{:T(128)}, bf16[64,2048]{1,0:T(8,128)(2,1)S(1)}, s32[32,8]{1,0:T(8,128)S(1)}, bf16[64,64,128]{2,0,1:T(8,128)(2,1)}, bf16[64,64,128]{2,0,1:T(8,...) while((s32[]{:T(128)}, bf16[64,2048]{1,0:T(8,128)(2,1)S(1)}, ...), condition=%wide.region_4.6_spmd, body=%wide.region_3.5_spmd.sunk | while | flops 809502080 | bytes 13704617 | solution.py:66
  128.7 0.1 reshape.156
  128.8 2.0 gather_fusion
  130.8 0.9 constant_dynamic-slice_fusion.2
  131.7 0.1 copy.58
  131.9 2.4 %fusion.36 = f32[8,8,128,64]{2,3,1,0:T(8,128)} fusion(f32[64,8,64,1]{0,2,3,1:T(8,128)S(1)} %bitcast.85, bf16[8,8,64,128]{3,2,1,0:T(8,128)(2,1)S(1)} %bitcast.83, pred[8,8]{1,0:T(8,128)(4,1)S(1)} %get-tuple-element.277), kind=kOutput, calls=%fused_computation.6.clone.1 | convolution fusion | flops 403177472 | bytes 3276864 | tf_op jit(solution)/shard_map/while/body/eval_jaxpr/mgp,mglo->glpo/dot_general | solution.py:61
  134.2 2.0 gather_fusion.1
  136.2 3.4 %convolution_bitcast_fusion.2 = f32[64,8,8,64]{3,0,2,1:T(8,128)S(1)} fusion(f32[8,8,128,64]{2,3,1,0:T(8,128)} %fusion.36, bf16[8,8,64,128]{3,2,1,0:T(8,128)(2,1)S(1)} %bitcast.84, pred[8,8]{1,0:T(8,128)(4,1)S(1)} %get-tuple-element.277), kind=kOutput, calls=%fused_computation.5.clone.1 | convolution fusion | flops 403177472 | bytes 4194368 | tf_op jit(solution)/shard_map/while/body/eval_jaxpr/glpo,mglo,gl->mgp/dot_general | solution.py:62
  139.8 3.1 %fusion.37 = bf16[8,1,64,64]{3,1,2,0:T(2,128)(2,1)S(1)} fusion(f32[8,8,1,1]{1,2,3,0:T(1,128)S(1)} %copy.57, f32[64,8,8,64]{3,0,2,1:T(8,128)S(1)} %convolution_bitcast_fusion.2), kind=kOutput, calls=%fused_computation.3.clone.1 | convolution fusion | flops 3145728 | bytes 1114368 | tf_op jit(solution)/shard_map/while/body/eval_jaxpr/glpo,mglo,gl->mgp/dot_general | solution.py:62
  142.9 0.2 copy.59
  143.1 0.1 reshape.157
  143.3 0.1 reshape.156
  143.4 2.0 gather_fusion
  145.4 0.9 constant_dynamic-slice_fusion.2
  146.3 0.1 copy.58
  146.4 2.4 %fusion.36 = f32[8,8,128,64]{2,3,1,0:T(8,128)} fusion(f32[64,8,64,1]{0,2,3,1:T(8,128)S(1)} %bitcast.85, bf16[8,8,64,128]{3,2,1,0:T(8,128)(2,1)S(1)} %bitcast.83, pred[8,8]{1,0:T(8,128)(4,1)S(1)} %get-tuple-element.277), kind=kOutput, calls=%fused_computation.6.clone.1 | convolution fusion | flops 403177472 | bytes 3276864 | tf_op jit(solution)/shard_map/while/body/eval_jaxpr/mgp,mglo->glpo/dot_general | solution.py:61
  148.8 2.0 gather_fusion.1
  150.8 3.4 %convolution_bitcast_fusion.2 = f32[64,8,8,64]{3,0,2,1:T(8,128)S(1)} fusion(f32[8,8,128,64]{2,3,1,0:T(8,128)} %fusion.36, bf16[8,8,64,128]{3,2,1,0:T(8,128)(2,1)S(1)} %bitcast.84, pred[8,8]{1,0:T(8,128)(4,1)S(1)} %get-tuple-element.277), kind=kOutput, calls=%fused_computation.5.clone.1 | convolution fusion | flops 403177472 | bytes 4194368 | tf_op jit(solution)/shard_map/while/body/eval_jaxpr/glpo,mglo,gl->mgp/dot_general | solution.py:62
  154.4 3.1 %fusion.37 = bf16[8,1,64,64]{3,1,2,0:T(2,128)(2,1)S(1)} fusion(f32[8,8,1,1]{1,2,3,0:T(1,128)S(1)} %copy.57, f32[64,8,8,64]{3,0,2,1:T(8,128)S(1)} %convolution_bitcast_fusion.2), kind=kOutput, calls=%fused_computation.3.clone.1 | convolution fusion | flops 3145728 | bytes 1114368 | tf_op jit(solution)/shard_map/while/body/eval_jaxpr/glpo,mglo,gl->mgp/dot_general | solution.py:62
  157.5 0.2 copy.59
  157.7 0.1 reshape.157
  157.9 0.1 reshape.156
  158.0 2.0 gather_fusion
  159.9 0.9 constant_dynamic-slice_fusion.2
  160.9 0.1 copy.58
  161.0 2.4 %fusion.36 = f32[8,8,128,64]{2,3,1,0:T(8,128)} fusion(f32[64,8,64,1]{0,2,3,1:T(8,128)S(1)} %bitcast.85, bf16[8,8,64,128]{3,2,1,0:T(8,128)(2,1)S(1)} %bitcast.83, pred[8,8]{1,0:T(8,128)(4,1)S(1)} %get-tuple-element.277), kind=kOutput, calls=%fused_computation.6.clone.1 | convolution fusion | flops 403177472 | bytes 3276864 | tf_op jit(solution)/shard_map/while/body/eval_jaxpr/mgp,mglo->glpo/dot_general | solution.py:61
  163.4 2.0 gather_fusion.1
  165.4 3.4 %convolution_bitcast_fusion.2 = f32[64,8,8,64]{3,0,2,1:T(8,128)S(1)} fusion(f32[8,8,128,64]{2,3,1,0:T(8,128)} %fusion.36, bf16[8,8,64,128]{3,2,1,0:T(8,128)(2,1)S(1)} %bitcast.84, pred[8,8]{1,0:T(8,128)(4,1)S(1)} %get-tuple-element.277), kind=kOutput, calls=%fused_computation.5.clone.1 | convolution fusion | flops 403177472 | bytes 4194368 | tf_op jit(solution)/shard_map/while/body/eval_jaxpr/glpo,mglo,gl->mgp/dot_general | solution.py:62
  169.0 3.1 %fusion.37 = bf16[8,1,64,64]{3,1,2,0:T(2,128)(2,1)S(1)} fusion(f32[8,8,1,1]{1,2,3,0:T(1,128)S(1)} %copy.57, f32[64,8,8,64]{3,0,2,1:T(8,128)S(1)} %convolution_bitcast_fusion.2), kind=kOutput, calls=%fused_computation.3.clone.1 | convolution fusion | flops 3145728 | bytes 1114368 | tf_op jit(solution)/shard_map/while/body/eval_jaxpr/glpo,mglo,gl->mgp/dot_general | solution.py:62
  172.1 0.2 copy.59
  172.2 0.1 reshape.157
  172.4 0.1 reshape.156
  172.5 2.0 gather_fusion
  174.5 0.9 constant_dynamic-slice_fusion.2
  175.4 0.1 copy.58
  175.6 2.4 %fusion.36 = f32[8,8,128,64]{2,3,1,0:T(8,128)} fusion(f32[64,8,64,1]{0,2,3,1:T(8,128)S(1)} %bitcast.85, bf16[8,8,64,128]{3,2,1,0:T(8,128)(2,1)S(1)} %bitcast.83, pred[8,8]{1,0:T(8,128)(4,1)S(1)} %get-tuple-element.277), kind=kOutput, calls=%fused_computation.6.clone.1 | convolution fusion | flops 403177472 | bytes 3276864 | tf_op jit(solution)/shard_map/while/body/eval_jaxpr/mgp,mglo->glpo/dot_general | solution.py:61
  178.0 2.0 gather_fusion.1
  179.9 3.4 %convolution_bitcast_fusion.2 = f32[64,8,8,64]{3,0,2,1:T(8,128)S(1)} fusion(f32[8,8,128,64]{2,3,1,0:T(8,128)} %fusion.36, bf16[8,8,64,128]{3,2,1,0:T(8,128)(2,1)S(1)} %bitcast.84, pred[8,8]{1,0:T(8,128)(4,1)S(1)} %get-tuple-element.277), kind=kOutput, calls=%fused_computation.5.clone.1 | convolution fusion | flops 403177472 | bytes 4194368 | tf_op jit(solution)/shard_map/while/body/eval_jaxpr/glpo,mglo,gl->mgp/dot_general | solution.py:62
  183.5 3.1 %fusion.37 = bf16[8,1,64,64]{3,1,2,0:T(2,128)(2,1)S(1)} fusion(f32[8,8,1,1]{1,2,3,0:T(1,128)S(1)} %copy.57, f32[64,8,8,64]{3,0,2,1:T(8,128)S(1)} %convolution_bitcast_fusion.2), kind=kOutput, calls=%fused_computation.3.clone.1 | convolution fusion | flops 3145728 | bytes 1114368 | tf_op jit(solution)/shard_map/while/body/eval_jaxpr/glpo,mglo,gl->mgp/dot_general | solution.py:62
  186.6 0.2 copy.59
  186.8 0.1 reshape.157
  187.0 1.2 fusion.13
  188.2 0.5 copy.38
  188.8 32.7 %all_to_all.32 = f32[64,1,2048]{2,1,0:T(1,128)S(1)} all-to-all(f32[64,1,2048]{2,1,0:T(1,128)S(1)} %copy.38), channel_id=1, replica_groups=mesh['slab'=64,'obs'=8] {'slab'}, dimensions={0} | all-to-all | bytes 1048576 | tf_op jit(solution)/shard_map/all_to_all | solution.py:97
  221.4 0.8 copy.69
  (40 shorter events, 1.0 us)
Async XLA Ops:
  6.5 32.5 %all-to-all-start = ((f32[1,64,2048]{2,0,1:T(1,128)}), f32[1,64,2048]{2,0,1:T(1,128)S(1)}, u32[]{:S(2)}, u32[]{:S(2)}) async-start(f32[1,64,2048]{2,0,1:T(1,128)} %bitcast.93), calls=%async_computation | async-start | bytes 1048576 | tf_op jit(solution)/shard_map/all_to_all | solution.py:80
  21.4 60.4 %all-gather.3.cloned.1.call-start = ((), (), s32[]{:S(2)}) async-start(), calls=%async_computation.2 | async-start | bytes 2359296 | tf_op jit(solution)/shard_map/all_gather | solution.py:44
  39.1 0.8 copy-start
  40.1 4.3 %copy-start.2 = (f32[1,1024]{1,0:T(1,128)S(1)}, f32[1,1024]{1,0:T(1,128)}, u32[]{:S(2)}) copy-start(f32[1,1024]{1,0:T(1,128)} %param.15) | copy-start | bytes 12292
  40.1 4.3 %copy-start.1 = (f32[1,1024]{1,0:T(1,128)S(1)}, f32[1,1024]{1,0:T(1,128)}, u32[]{:S(2)}) copy-start(f32[1,1024]{1,0:T(1,128)} %param.14) | copy-start | bytes 12292
  40.1 6.7 %copy-start.3 = (s32[1,32,8]{1,2,0:T(8,128)S(1)}, s32[1,32,8]{1,2,0:T(8,128)}, u32[]{:S(2)}) copy-start(s32[1,32,8]{1,2,0:T(8,128)} %param.18) | copy-start | bytes 3076
  40.1 6.8 %copy-start.4 = (f32[1,32,8]{1,2,0:T(8,128)S(1)}, f32[1,32,8]{1,2,0:T(8,128)}, u32[]{:S(2)}) copy-start(f32[1,32,8]{1,2,0:T(8,128)} %param.19) | copy-start | bytes 3076
  46.1 79.9 %all-gather.5.cloned.1.call-start = ((), (), s32[]{:S(2)}) async-start(), calls=%async_computation.3 | async-start | bytes 2359296 | tf_op jit(solution)/shard_map/all_gather | solution.py:43
Sparse Core Ops, SparseCore 0:
  46.2 35.5 all-gather.2
  83.8 42.0 all-gather.4
where the time goes:
time: 230 us; the launch traced here: 229 us
  waiting for transfers between devices  90.7 us (39%)
  matrix products  35.7 us (16%)
  local copies, waits for them, and re-layouts  33.9 us (15%)
  blocking collectives  32.7 us (14%)
  starting transfers between devices  14.9 us (6%)
  between operations  14.2 us (6%)
  other arithmetic  6.66 us (3%)
    all_gather x1, waiting for transfers between devices, compute_increment(): lax.all_gather(prior_low, 'obs', axis=1, tiled=True)  41.5 us
    all_gather x1, waiting for transfers between devices, compute_increment(): lax.all_gather(gain_input, 'obs', axis=1, tiled=True)  33.9 us
    all_to_all x1, blocking collectives, local(): lax.all_to_all(analysis, 'slab', split_axis=0, concat_axis=1, tiled=True)  32.7 us
    dot_general x8, matrix products, one_group(): jnp.einsum('glpo,mglo,gl->mgp', covariance, picked_gain, scales, precisio...  26.2 us
    all_to_all x1, starting transfers between devices, local(): lax.all_to_all(background_members, 'slab', split_axis=1, concat_axis=0, t...  14.8 us
    all_to_all x1, waiting for transfers between devices, local(): lax.all_to_all(background_members, 'slab', split_axis=1, concat_axis=0, t...  14.5 us
    dot_general x4, matrix products, one_group(): jnp.einsum('mgp,mglo->glpo', local_dev, picked_prior, precision=highest)  9.56 us
    gather x4, local copies, waits for them, and re-layouts, one_group(): picked_prior = jnp.take(all_prior, chosen, axis=1).astype(jnp.float32)  7.9 us
  transfers between devices with their start and end apart: 3, of which 3 were waited for; matrix products, arithmetic and copies ran while one was open for 3% of the time, Pallas kernels for 0%

commit v1 on v0

v1 whole, which is shorter than its diff:
```python
import jax
import jax.numpy as jnp
from jax import lax
from jax.sharding import PartitionSpec as P

OB = 128


highest = lax.Precision.HIGHEST


def block_products(
    tile_work,
    measurement_jitter,
    measurement_readings,
    measurement_noise_spread,
    measurement_grid_location,
    active_tallies,
):
    members = tile_work.shape[0]
    positions = measurement_grid_location[0]
    obs_count = positions.shape[0]
    prior_value = jnp.take(tile_work, positions, axis=1)
    prior_shift = prior_value - jnp.mean(prior_value, axis=0, keepdims=True)
    spread = jnp.sum(prior_shift * prior_shift, axis=0, keepdims=True) / (members - 1)
    usable = jnp.arange(obs_count, dtype=jnp.int32)[None, :] < active_tallies[0, 0]
    innovation = (
        measurement_readings + measurement_jitter[:, 0, :].astype(jnp.float32) - prior_value
    ) / (spread + measurement_noise_spread)
    gain_input = jnp.where(usable, innovation, jnp.float32(0.0)).astype(jnp.bfloat16)
    prior_low = prior_shift.astype(jnp.bfloat16)
    return jnp.einsum(
        "mco,nco->cmn",
        gain_input.reshape(members, -1, OB),
        prior_low.reshape(members, -1, OB),
        preferred_element_type=jnp.float32,
    )


def local(
    background_members,
    measurement_jitter,
    measurement_readings,
    measurement_noise_spread,
    measurement_grid_location,
    active_tallies,
    coupling_listing,
    taper_factors,
):
    work_low = background_members.astype(jnp.bfloat16)
    tile_low = lax.all_to_all(work_low, "slab", split_axis=1, concat_axis=0, tiled=True)
    tile_work = tile_low.astype(jnp.float32)
    members = tile_work.shape[0]
    blocks = coupling_listing.shape[1]
    deviation = tile_work - jnp.mean(tile_work, axis=0, keepdims=True)

    products = block_products(
        tile_work,
        measurement_jitter,
        measurement_readings,
        measurement_noise_spread,
        measurement_grid_location,
        active_tallies,
    )
    all_products = lax.all_gather(products, "obs", axis=0, tiled=True)
    obs_blocks = all_products.shape[0]

    block_links = coupling_listing[0]
    factor = taper_factors[0] / (members - 1)
    choose = block_links[..., None] == jnp.arange(obs_blocks, dtype=jnp.int32)
    localize = jnp.sum(jnp.where(choose, factor[..., None], jnp.float32(0.0)), axis=1)
    ensemble = jnp.einsum("bc,cmn->bmn", localize, all_products, precision=highest)
    region_dev = deviation.reshape(members, blocks, -1)
    increment = jnp.einsum("bmn,nbp->mbp", ensemble, region_dev, precision=highest)
    increment_low = increment.reshape(members, -1).astype(jnp.bfloat16)
    back = lax.all_to_all(increment_low, "slab", split_axis=0, concat_axis=1, tiled=True)
    return background_members + back.astype(jnp.float32)


def solution(mesh):
    return jax.shard_map(
        local,
        mesh=mesh,
        in_specs=(
            P("slab", "obs"),
            P(None, "obs", "slab"),
            P("obs", "slab"),
            P("obs", "slab"),
            P("obs", "slab"),
            P("obs", "slab"),
            P("obs", "slab", None),
            P("obs", "slab", None),
        ),
        out_specs=P("slab", "obs"),
        check_vma=False,
    )
```

time: 230 us -> 125 us (0.54)
  waiting for transfers between devices: 90.7 us -> 46.4 us
  matrix products: 35.7 us -> 7.11 us
  local copies, waits for them, and re-layouts: 33.9 us -> 6.04 us
  blocking collectives: 32.7 us -> 28.1 us
    all_gather x2 -> x1, waiting for transfers between devices: 75.5 us -> 34.1 us  [local(): all_products = lax.all_gather(products, 'obs', axis=0, tiled=True)]
    dot_general x12 -> x3, matrix products: 35.7 us -> 7.11 us  [the longest x1 3.85 us: local(): jnp.einsum('bc,cmn->bmn', localize, all_products, precision=highest)]
    gather x9 -> x2, local copies, waits for them, and re-layouts: 18.6 us -> 2.99 us  [block_products(): prior_value = jnp.take(tile_work, positions, axis=1)]
    while x2 -> x0, local copies, waits for them, and re-layouts: 5.37 us -> none  [compute_increment(): lax.fori_loop(0, group_count, one_group, jnp.zeros_like(deviation))]
    dynamic_slice x16 -> x0, local copies, waits for them, and re-layouts: 4.76 us -> none  [the longest x8 4.16 us: one_group(): lax.dynamic_slice_in_dim(deviation, first_block * block_width, group_size...]
    all_to_all x1, blocking collectives: 32.7 us -> 28.1 us  [local(): lax.all_to_all(increment_low, 'slab', split_axis=0, concat_axis=1, tiled=...]
  transfers between devices with their start and end apart: 3 -> 2, of which waited for: 3 -> 2; matrix products, arithmetic and copies ran while one was open for 3% -> 1% of each run, Pallas kernels for 0% -> 0%
where the time goes in v1:
time: 125 us; the launch traced here: 124 us
  waiting for transfers between devices  46.4 us (37%)
  blocking collectives  28.1 us (22%)
  starting transfers between devices  14.9 us (12%)
  between operations  14.3 us (11%)
  other arithmetic  7.54 us (6%)
  matrix products  7.11 us (6%)
  local copies, waits for them, and re-layouts  6.04 us (5%)
    all_gather x1, waiting for transfers between devices, local(): all_products = lax.all_gather(products, 'obs', axis=0, tiled=True)  34.1 us
    all_to_all x1, blocking collectives, local(): lax.all_to_all(increment_low, 'slab', split_axis=0, concat_axis=1, tiled=...  28.1 us
    all_to_all x1, starting transfers between devices, local(): lax.all_to_all(work_low, 'slab', split_axis=1, concat_axis=0, tiled=True)  14.8 us
    all_to_all x1, waiting for transfers between devices, local(): lax.all_to_all(work_low, 'slab', split_axis=1, concat_axis=0, tiled=True)  12.2 us
    dot_general x1, matrix products, local(): jnp.einsum('bc,cmn->bmn', localize, all_products, precision=highest)  3.85 us
    gather x2, local copies, waits for them, and re-layouts, block_products(): prior_value = jnp.take(tile_work, positions, axis=1)  2.99 us
  transfers between devices with their start and end apart: 2, of which 2 were waited for; matrix products, arithmetic and copies ran while one was open for 1% of the time, Pallas kernels for 0%

profile of v1, /device:TPU:1, one launch (start us, length us, event | category | flops | bytes accessed | tf_op | source)
XLA Modules:
  0.0 124.3 jit_solution(9766494422847316278)
XLA Ops:
  6.5 0.0 copy-start.1
  6.5 0.0 copy-start.2
  6.5 1.4 %convert_element_type.60 = bf16[1,131072]{1,0:T(2,128)(2,1)S(1)} convert(f32[1,131072]{1,0:T(1,128)} %param.8) | non-fusion elementwise | flops 131072 | bytes 786432 | tf_op jit(solution)/shard_map/convert_element_type | solution.py:50
  8.0 0.5 broadcast.91
  8.5 2.1 %reduce.1 = bf16[64,2048]{1,0:T(8,128)(2,1)S(1)} reduce(bf16[64,1,2048]{2,1,0:T(2,128)(2,1)S(1)} %bitcast.46, bf16[]{:T(256)} %broadcast.91), dimensions={1}, to_apply=%bitcast.40.reduce_sub_computation | reduce | bytes 524290
  10.6 0.9 reshape.167
  11.5 14.8 %all-to-all-start = ((bf16[64,2,1024]{2,1,0:T(2,128)(2,1)}), bf16[64,2,1024]{2,1,0:T(2,128)(2,1)S(1)}, u32[]{:S(2)}, u32[]{:S(2)}) async-start(bf16[64,2,1024]{2,1,0:T(2,128)(2,1)} %reshape.167), calls=%async_computation | async-start | bytes 524288 | tf_op jit(solution)/shard_map/all_to_all | solution.py:51
  26.3 0.0 all-gather.2.cloned.1.call-start
  27.0 0.0 copy-done.1
  27.1 0.0 copy-done.2
  27.2 12.2 %all-to-all-done = bf16[64,2,1024]{2,1,0:T(2,128)(2,1)S(1)} async-done(((bf16[64,2,1024]{2,1,0:T(2,128)(2,1)}), bf16[64,2,1024]{2,1,0:T(2,128)(2,1)S(1)}, u32[]{:S(2)}, u32[]{:S(2)}) %all-to-all-start) | async-done | bytes 262176 | tf_op jit(solution)/shard_map/all_to_all | solution.py:51
  39.4 0.2 reshape.168
  39.7 0.5 copy.28
  40.2 0.1 convert_bitcast_fusion
  40.3 0.0 copy-start.3
  40.3 0.0 copy-start.6
  40.3 2.8 %gather_fusion = f32[1024,64]{1,0:T(8,128)S(1)} fusion(f32[64,2048]{0,1:T(8,128)S(1)} %convert_bitcast_fusion, s32[1024]{0:T(1024)S(1)} %broadcast_clamp_fusion), kind=kCustom, calls=%fused_computation | custom fusion | bytes 528384 | tf_op jit(solution)/shard_map/jit(_take)/gather | solution.py:23
  43.1 0.0 copy-start.5
  43.1 0.0 copy-start.4
  43.1 0.4 fusion.5
  43.5 0.5 multiply_reduce_fusion
  44.0 0.2 copy.32
  44.2 0.0 copy-done.3
  44.2 0.0 copy-done.6
  44.2 0.9 fusion.10
  45.2 0.0 all-gather.2.cloned.1.call-update
  45.2 0.0 copy-done.5
  45.2 0.1 copy.30
  45.3 0.0 copy-done.4
  45.3 0.1 copy.29
  45.4 0.1 select_reduce_fusion
  45.5 0.2 convert_reduce_fusion
  45.7 0.1 div.45
  45.8 34.1 %all-gather.2.cloned.1.call-done = f32[64,64,64]{2,1,0:T(8,128)} async-done(((f32[8,64,64]{2,1,0:T(8,128)}), f32[64,64,64]{2,1,0:T(8,128)}) %all-gather.2.cloned.1.call-update) | async-done | bytes 1048592 | tf_op jit(solution)/shard_map/all_gather | solution.py:65
  80.0 3.9 %fusion = f32[32,64,64]{2,0,1:T(8,128)S(1)} fusion(f32[64,64,64]{2,1,0:T(8,128)} %all-gather.2.cloned.1.call-done, f32[32,64]{1,0:T(8,128)S(1)} %select_reduce_fusion), kind=kOutput, calls=%fused_computation.1 | convolution fusion | flops 100663296 | bytes 1581056 | tf_op jit(solution)/shard_map/bc,cmn->bmn/dot_general | solution.py:72
  83.8 2.3 %convolution_convert_fusion = bf16[32,64,64]{2,1,0:T(8,128)(2,1)S(1)} fusion(f32[32,64,64]{2,0,1:T(8,128)S(1)} %fusion, f32[32,64]{1,0:T(8,128)S(1)} %div.45, bf16[64,32,64]{0,2,1:T(8,128)(2,1)S(1)} %bitcast.43), kind=kOutput, calls=%fused_computation.3 | convolution fusion | flops 101056512 | bytes 1056768 | tf_op jit(solution)/shard_map/bmn,nbp->mbp/dot_general | solution.py:74
  86.2 0.0 copy-start
  86.2 1.1 reduce.2
  87.3 0.2 copy.51
  87.5 0.2 reshape.169
  87.7 28.1 %all_to_all.23 = bf16[64,2,1024]{2,1,0:T(2,128)(2,1)S(1)} all-to-all(bf16[64,2,1024]{2,1,0:T(2,128)(2,1)S(1)} %reshape.169), channel_id=1, replica_groups=mesh['slab'=64,'obs'=8] {'slab'}, dimensions={0} | all-to-all | bytes 524288 | tf_op jit(solution)/shard_map/all_to_all | solution.py:76
  115.8 0.2 reshape.170
  116.0 0.0 copy-done
  116.0 1.5 %convert_add_fusion = f32[1,131072]{1,0:T(1,128)} fusion(f32[1,131072]{1,0:T(1,128)S(1)} %copy-done, bf16[1,131072]{1,0:T(2,128)(2,1)S(1)} %bitcast.45), kind=kLoop, calls=%fused_computation.6 | loop fusion | flops 262144 | bytes 1310720 | tf_op jit(solution)/shard_map/add | solution.py:77
  (11 shorter events, 0.1 us)
Async XLA Ops:
  6.5 20.5 %copy-start.1 = (bf16[64,1,1024]{2,0,1:T(8,128)(2,1)S(1)}, bf16[64,1,1024]{2,0,1:T(8,128)(2,1)}, u32[]{:S(2)}) copy-start(bf16[64,1,1024]{2,0,1:T(8,128)(2,1)} %param.9) | copy-start | bytes 393220
  6.5 20.5 %copy-start.2 = (s32[1,1024]{1,0:T(1,128)S(1)}, s32[1,1024]{1,0:T(1,128)}, u32[]{:S(2)}) copy-start(s32[1,1024]{1,0:T(1,128)} %param.12) | copy-start | bytes 12292
  11.5 27.9 %all-to-all-start = ((bf16[64,2,1024]{2,1,0:T(2,128)(2,1)}), bf16[64,2,1024]{2,1,0:T(2,128)(2,1)S(1)}, u32[]{:S(2)}, u32[]{:S(2)}) async-start(bf16[64,2,1024]{2,1,0:T(2,128)(2,1)} %reshape.167), calls=%async_computation | async-start | bytes 524288 | tf_op jit(solution)/shard_map/all_to_all | solution.py:51
  26.3 53.6 %all-gather.2.cloned.1.call-start = ((), (), s32[]{:S(2)}) async-start(), calls=%async_computation.2 | async-start | bytes 2359296 | tf_op jit(solution)/shard_map/all_gather | solution.py:65
  40.3 4.0 %copy-start.3 = (f32[1,1024]{1,0:T(1,128)S(1)}, f32[1,1024]{1,0:T(1,128)}, u32[]{:S(2)}) copy-start(f32[1,1024]{1,0:T(1,128)} %param.11) | copy-start | bytes 12292
  40.3 4.0 %copy-start.6 = (f32[1,1024]{1,0:T(1,128)S(1)}, f32[1,1024]{1,0:T(1,128)}, u32[]{:S(2)}) copy-start(f32[1,1024]{1,0:T(1,128)} %param.10) | copy-start | bytes 12292
  43.1 2.1 %copy-start.5 = (f32[1,32,8]{1,2,0:T(8,128)S(1)}, f32[1,32,8]{1,2,0:T(8,128)}, u32[]{:S(2)}) copy-start(f32[1,32,8]{1,2,0:T(8,128)} %param.15) | copy-start | bytes 3076
  43.1 2.2 %copy-start.4 = (s32[1,32,8]{1,2,0:T(8,128)S(1)}, s32[1,32,8]{1,2,0:T(8,128)}, u32[]{:S(2)}) copy-start(s32[1,32,8]{1,2,0:T(8,128)} %param.14) | copy-start | bytes 3076
  86.2 29.8 %copy-start = (f32[1,131072]{1,0:T(1,128)S(1)}, f32[1,131072]{1,0:T(1,128)}, u32[]{:S(2)}) copy-start(f32[1,131072]{1,0:T(1,128)} %param.8) | copy-start | bytes 1572868
Sparse Core Ops, SparseCore 0:
  45.3 34.6 all-gather.1

commit v2 on v1

--- a/solution.py
+++ b/solution.py
@@ -62,7 +62,10 @@
         measurement_grid_location,
         active_tallies,
     )
-    all_products = lax.all_gather(products, "obs", axis=0, tiled=True)
+    groups = lax.axis_size("obs")
+    copies = jnp.broadcast_to(products[None], (groups,) + products.shape)
+    all_products = lax.all_to_all(copies, "obs", split_axis=0, concat_axis=0, tiled=True)
+    all_products = all_products.reshape((-1,) + products.shape[1:])
     obs_blocks = all_products.shape[0]
 
     block_links = coupling_listing[0]

time: 125 us -> 108 us (0.86)
  between operations: 14.3 us -> 0.95 us
  blocking collectives: 28.1 us -> 17.6 us
  starting transfers between devices: 14.9 us -> 21.6 us
  waiting for transfers between devices: 46.4 us -> 40.9 us
  local copies, waits for them, and re-layouts: 6.04 us -> 11.1 us
  other arithmetic: 7.54 us -> 12.2 us
  matrix products: 7.11 us -> 3.67 us
    all_gather x1 -> x0, waiting for transfers between devices: 34.1 us -> none  [local(): all_products = lax.all_gather(products, 'obs', axis=0, tiled=True)]
    all_to_all x0 -> x1, waiting for transfers between devices: none -> 28.6 us  [local(): lax.all_to_all(copies, 'obs', split_axis=0, concat_axis=0, tiled=True)]
    all_to_all x1, blocking collectives: 28.1 us -> 17.6 us  [local(): lax.all_to_all(increment_low, 'slab', split_axis=0, concat_axis=1, tiled=...]
    all_to_all x0 -> x1, starting transfers between devices: none -> 6.82 us  [local(): lax.all_to_all(copies, 'obs', split_axis=0, concat_axis=0, tiled=True)]
    all_to_all x0 -> x1, other arithmetic: none -> 4.52 us  [local(): lax.all_to_all(copies, 'obs', split_axis=0, concat_axis=0, tiled=True)]
    unnamed x21 -> x24, local copies, waits for them, and re-layouts: 2.31 us -> 6.72 us
    dot_general x1, matrix products: 3.85 us -> 1.11 us  [local(): jnp.einsum('bc,cmn->bmn', localize, all_products, precision=highest)]
where the time goes in v2:
time: 108 us
  waiting for transfers between devices  40.9 us (38%)
  starting transfers between devices  21.6 us (20%)
  blocking collectives  17.6 us (16%)
  other arithmetic  12.2 us (11%)
  local copies, waits for them, and re-layouts  11.1 us (10%)
  matrix products  3.67 us (3%)
    all_to_all x1, waiting for transfers between devices, local(): lax.all_to_all(copies, 'obs', split_axis=0, concat_axis=0, tiled=True)  28.6 us
    all_to_all x1, blocking collectives, local(): lax.all_to_all(increment_low, 'slab', split_axis=0, concat_axis=1, tiled=...  17.6 us
    all_to_all x1, starting transfers between devices, local(): lax.all_to_all(work_low, 'slab', split_axis=1, concat_axis=0, tiled=True)  14.8 us
    all_to_all x1, waiting for transfers between devices, local(): lax.all_to_all(work_low, 'slab', split_axis=1, concat_axis=0, tiled=True)  12.3 us
    all_to_all x1, starting transfers between devices, local(): lax.all_to_all(copies, 'obs', split_axis=0, concat_axis=0, tiled=True)  6.82 us
    unnamed x24, local copies, waits for them, and re-layouts  6.72 us
    all_to_all x1, other arithmetic, local(): lax.all_to_all(copies, 'obs', split_axis=0, concat_axis=0, tiled=True)  4.52 us
    gather x2, local copies, waits for them, and re-layouts, block_products(): prior_value = jnp.take(tile_work, positions, axis=1)  2.99 us
  transfers between devices with their start and end apart: 2, of which 2 were waited for; matrix products, arithmetic and copies ran while one was open for 1% of the time, Pallas kernels for 0%

profile of v2, /device:TPU:1, one launch (start us, length us, event | category | flops | bytes accessed | tf_op | source)
XLA Modules:
  0.0 108.1 jit_solution(8541478088746418677)
XLA Ops:
  0.0 0.0 copy-start.1
  0.0 0.0 copy-start.2
  0.0 1.4 %convert_element_type.60 = bf16[1,131072]{1,0:T(2,128)(2,1)S(1)} convert(f32[1,131072]{1,0:T(1,128)} %param.8) | non-fusion elementwise | flops 131072 | bytes 786432 | tf_op jit(solution)/shard_map/convert_element_type | solution.py:50
  1.4 0.6 broadcast.92
  2.0 2.2 %reduce.1 = bf16[64,2048]{1,0:T(8,128)(2,1)S(1)} reduce(bf16[64,1,2048]{2,1,0:T(2,128)(2,1)S(1)} %bitcast.55, bf16[]{:T(256)} %broadcast.92), dimensions={1}, to_apply=%bitcast.43.reduce_sub_computation | reduce | bytes 524290
  4.2 0.9 reshape.172
  5.1 14.8 %all-to-all-start = ((bf16[64,2,1024]{2,1,0:T(2,128)(2,1)}), bf16[64,2,1024]{2,1,0:T(2,128)(2,1)S(1)}, u32[]{:S(2)}, u32[]{:S(2)}) async-start(bf16[64,2,1024]{2,1,0:T(2,128)(2,1)} %reshape.172), calls=%async_computation | async-start | bytes 524288 | tf_op jit(solution)/shard_map/all_to_all | solution.py:51
  20.6 0.0 copy-done.1
  20.6 0.0 copy-done.2
  20.8 12.3 %all-to-all-done = bf16[64,2,1024]{2,1,0:T(2,128)(2,1)S(1)} async-done(((bf16[64,2,1024]{2,1,0:T(2,128)(2,1)}), bf16[64,2,1024]{2,1,0:T(2,128)(2,1)S(1)}, u32[]{:S(2)}, u32[]{:S(2)}) %all-to-all-start) | async-done | bytes 262176 | tf_op jit(solution)/shard_map/all_to_all | solution.py:51
  33.0 0.2 reshape.173
  33.3 0.5 copy.40
  33.8 0.1 convert_bitcast_fusion
  33.9 0.0 copy-start.3
  33.9 0.0 copy-start.6
  33.9 2.8 %gather_fusion = f32[1024,64]{1,0:T(8,128)S(1)} fusion(f32[64,2048]{0,1:T(8,128)S(1)} %convert_bitcast_fusion, s32[1024]{0:T(1024)S(1)} %broadcast_clamp_fusion), kind=kCustom, calls=%fused_computation | custom fusion | bytes 528384 | tf_op jit(solution)/shard_map/jit(_take)/gather | solution.py:23
  36.7 0.4 fusion.6
  37.1 0.5 multiply_reduce_fusion
  37.6 0.2 copy.44
  37.8 0.0 copy-done.3
  37.8 0.0 copy-done.6
  37.8 0.2 fusion.11
  38.0 0.2 copy.45
  38.2 0.1 broadcast_bitcast_fusion
  38.4 0.0 copy-start.5
  38.4 0.0 copy-start.4
  38.4 2.1 %reshape.174 = f32[8,1,32768]{2,1,0:T(1,128)} reshape(f32[8,64,8,64]{3,2,1,0:T(8,128)S(1)} %broadcast_bitcast_fusion) | data formatting | bytes 2097152
  40.5 6.8 %all-to-all-start.1 = ((f32[8,1,32768]{2,1,0:T(1,128)}), f32[8,1,32768]{2,1,0:T(1,128)S(1)}, u32[]{:S(2)}, u32[]{:S(2)}) async-start(f32[8,1,32768]{2,1,0:T(1,128)} %reshape.174), calls=%async_computation.1 | async-start | bytes 2097152 | tf_op jit(solution)/shard_map/all_to_all | solution.py:67
  47.3 0.0 copy-done.5
  47.4 0.1 copy.42
  47.4 0.0 copy-done.4
  47.4 0.1 copy.41
  47.5 0.1 select_reduce_fusion
  47.7 0.2 convert_reduce_fusion
  47.9 0.1 div.45
  48.0 28.6 %all-to-all-done.1 = f32[8,1,32768]{2,1,0:T(1,128)S(1)} async-done(((f32[8,1,32768]{2,1,0:T(1,128)}), f32[8,1,32768]{2,1,0:T(1,128)S(1)}, u32[]{:S(2)}, u32[]{:S(2)}) %all-to-all-start.1) | async-done | bytes 1048608 | tf_op jit(solution)/shard_map/all_to_all | solution.py:67
  76.6 0.5 broadcast.93
  77.1 4.5 %reduce.2 = f32[8,32768]{1,0:T(8,128)} reduce(f32[8,1,32768]{2,1,0:T(1,128)S(1)} %all-to-all-done.1, f32[]{:T(128)} %broadcast.93), dimensions={1}, to_apply=%all_to_all.23.reduce_sub_computation | reduce | bytes 2097156 | tf_op jit(solution)/shard_map/all_to_all | solution.py:67
  81.6 2.1 %reshape.175 = f32[8,64,8,64]{3,2,1,0:T(8,128)S(1)} reshape(f32[8,32768]{1,0:T(8,128)} %reduce.2) | data formatting | bytes 2097152
  83.7 1.1 %fusion = f32[32,64,64]{2,0,1:T(8,128)S(1)} fusion(f32[32,64]{1,0:T(8,128)S(1)} %select_reduce_fusion, f32[8,64,8,64]{3,2,1,0:T(8,128)S(1)} %reshape.175), kind=kOutput, calls=%fused_computation.1 | convolution fusion | flops 100663296 | bytes 1581056 | tf_op jit(solution)/shard_map/bc,cmn->bmn/dot_general | solution.py:75
  84.8 2.3 %convolution_convert_fusion = bf16[32,64,64]{2,1,0:T(8,128)(2,1)S(1)} fusion(f32[32,64,64]{2,0,1:T(8,128)S(1)} %fusion, f32[32,64]{1,0:T(8,128)S(1)} %div.45, bf16[64,32,64]{0,2,1:T(8,128)(2,1)S(1)} %bitcast.52), kind=kOutput, calls=%fused_computation.4 | convolution fusion | flops 101056512 | bytes 1056768 | tf_op jit(solution)/shard_map/bmn,nbp->mbp/dot_general | solution.py:77
  87.2 0.0 copy-start
  87.2 1.2 %reduce.3 = bf16[64,2048]{0,1:T(8,128)(2,1)S(1)} reduce(bf16[64,1,2048]{0,2,1:T(8,128)(2,1)S(1)} %bitcast.57, bf16[]{:T(256)} %broadcast.92), dimensions={1}, to_apply=%copy.48.reduce_sub_computation | reduce | bytes 524290 | tf_op jit(solution)/shard_map/convert_element_type | solution.py:78
  88.4 0.2 copy.66
  88.6 0.2 reshape.176
  88.8 17.6 %all_to_all.28 = bf16[64,2,1024]{2,1,0:T(2,128)(2,1)S(1)} all-to-all(bf16[64,2,1024]{2,1,0:T(2,128)(2,1)S(1)} %reshape.176), channel_id=1, replica_groups=mesh['slab'=64,'obs'=8] {'slab'}, dimensions={0} | all-to-all | bytes 524288 | tf_op jit(solution)/shard_map/all_to_all | solution.py:79
  106.4 0.2 reshape.177
  106.6 0.0 copy-done
  106.6 1.5 %convert_add_fusion = f32[1,131072]{1,0:T(1,128)} fusion(f32[1,131072]{1,0:T(1,128)S(1)} %copy-done, bf16[1,131072]{1,0:T(2,128)(2,1)S(1)} %bitcast.54), kind=kLoop, calls=%fused_computation.7 | loop fusion | flops 262144 | bytes 1310720 | tf_op jit(solution)/shard_map/add | solution.py:80
  (11 shorter events, 0.1 us)
Async XLA Ops:
  0.0 20.6 %copy-start.1 = (bf16[64,1,1024]{2,0,1:T(8,128)(2,1)S(1)}, bf16[64,1,1024]{2,0,1:T(8,128)(2,1)}, u32[]{:S(2)}) copy-start(bf16[64,1,1024]{2,0,1:T(8,128)(2,1)} %param.9) | copy-start | bytes 393220
  0.0 20.6 %copy-start.2 = (s32[1,1024]{1,0:T(1,128)S(1)}, s32[1,1024]{1,0:T(1,128)}, u32[]{:S(2)}) copy-start(s32[1,1024]{1,0:T(1,128)} %param.12) | copy-start | bytes 12292
  5.1 27.9 %all-to-all-start = ((bf16[64,2,1024]{2,1,0:T(2,128)(2,1)}), bf16[64,2,1024]{2,1,0:T(2,128)(2,1)S(1)}, u32[]{:S(2)}, u32[]{:S(2)}) async-start(bf16[64,2,1024]{2,1,0:T(2,128)(2,1)} %reshape.172), calls=%async_computation | async-start | bytes 524288 | tf_op jit(solution)/shard_map/all_to_all | solution.py:51
  33.9 3.9 %copy-start.3 = (f32[1,1024]{1,0:T(1,128)S(1)}, f32[1,1024]{1,0:T(1,128)}, u32[]{:S(2)}) copy-start(f32[1,1024]{1,0:T(1,128)} %param.11) | copy-start | bytes 12292
  33.9 3.9 %copy-start.6 = (f32[1,1024]{1,0:T(1,128)S(1)}, f32[1,1024]{1,0:T(1,128)}, u32[]{:S(2)}) copy-start(f32[1,1024]{1,0:T(1,128)} %param.10) | copy-start | bytes 12292
  38.4 9.0 %copy-start.5 = (f32[1,32,8]{1,2,0:T(8,128)S(1)}, f32[1,32,8]{1,2,0:T(8,128)}, u32[]{:S(2)}) copy-start(f32[1,32,8]{1,2,0:T(8,128)} %param.15) | copy-start | bytes 3076
  38.4 9.1 %copy-start.4 = (s32[1,32,8]{1,2,0:T(8,128)S(1)}, s32[1,32,8]{1,2,0:T(8,128)}, u32[]{:S(2)}) copy-start(s32[1,32,8]{1,2,0:T(8,128)} %param.14) | copy-start | bytes 3076
  40.5 36.1 %all-to-all-start.1 = ((f32[8,1,32768]{2,1,0:T(1,128)}), f32[8,1,32768]{2,1,0:T(1,128)S(1)}, u32[]{:S(2)}, u32[]{:S(2)}) async-start(f32[8,1,32768]{2,1,0:T(1,128)} %reshape.174), calls=%async_computation.1 | async-start | bytes 2097152 | tf_op jit(solution)/shard_map/all_to_all | solution.py:67
  87.2 19.4 %copy-start = (f32[1,131072]{1,0:T(1,128)S(1)}, f32[1,131072]{1,0:T(1,128)}, u32[]{:S(2)}) copy-start(f32[1,131072]{1,0:T(1,128)} %param.8) | copy-start | bytes 1572868

commit v3 on v2

--- a/solution.py
+++ b/solution.py
@@ -47,10 +47,11 @@
     coupling_listing,
     taper_factors,
 ):
-    work_low = background_members.astype(jnp.bfloat16)
-    tile_low = lax.all_to_all(work_low, "slab", split_axis=1, concat_axis=0, tiled=True)
-    tile_work = tile_low.astype(jnp.float32)
-    members = tile_work.shape[0]
+    members = lax.axis_size("slab")
+    lanes = 128
+    work_low = background_members.reshape(members, -1, lanes).astype(jnp.bfloat16)
+    tile_low = lax.all_to_all(work_low, "slab", split_axis=0, concat_axis=0, tiled=True)
+    tile_work = tile_low.reshape(members, -1).astype(jnp.float32)
     blocks = coupling_listing.shape[1]
     deviation = tile_work - jnp.mean(tile_work, axis=0, keepdims=True)
 
@@ -63,21 +64,22 @@
         active_tallies,
     )
     groups = lax.axis_size("obs")
-    copies = jnp.broadcast_to(products[None], (groups,) + products.shape)
+    flat = products.astype(jnp.bfloat16).reshape(products.shape[0], -1)
+    copies = jnp.broadcast_to(flat[None], (groups,) + flat.shape)
     all_products = lax.all_to_all(copies, "obs", split_axis=0, concat_axis=0, tiled=True)
-    all_products = all_products.reshape((-1,) + products.shape[1:])
+    all_products = all_products.reshape(-1, flat.shape[1]).astype(jnp.float32)
     obs_blocks = all_products.shape[0]
 
     block_links = coupling_listing[0]
     factor = taper_factors[0] / (members - 1)
     choose = block_links[..., None] == jnp.arange(obs_blocks, dtype=jnp.int32)
     localize = jnp.sum(jnp.where(choose, factor[..., None], jnp.float32(0.0)), axis=1)
-    ensemble = jnp.einsum("bc,cmn->bmn", localize, all_products, precision=highest)
+    ensemble = jnp.dot(localize, all_products, precision=highest).reshape(blocks, members, members)
     region_dev = deviation.reshape(members, blocks, -1)
     increment = jnp.einsum("bmn,nbp->mbp", ensemble, region_dev, precision=highest)
-    increment_low = increment.reshape(members, -1).astype(jnp.bfloat16)
-    back = lax.all_to_all(increment_low, "slab", split_axis=0, concat_axis=1, tiled=True)
-    return background_members + back.astype(jnp.float32)
+    increment_low = increment.reshape(members, -1, lanes).astype(jnp.bfloat16)
+    back = lax.all_to_all(increment_low, "slab", split_axis=0, concat_axis=0, tiled=True)
+    return background_members + back.reshape(background_members.shape).astype(jnp.float32)
 
 
 def solution(mesh):

time: 108 us -> 89.3 us (0.83)
  waiting for transfers between devices: 40.9 us -> 29.1 us
  other arithmetic: 12.2 us -> 5.62 us
  local copies, waits for them, and re-layouts: 11.1 us -> 8.15 us
  matrix products: 3.67 us -> 5.53 us
    all_to_all x1, waiting for transfers between devices: 28.6 us -> 17.5 us  [local(): lax.all_to_all(copies, 'obs', split_axis=0, concat_axis=0, tiled=True)]
    all_to_all x1 -> x0, other arithmetic: 4.52 us -> none  [local(): lax.all_to_all(copies, 'obs', split_axis=0, concat_axis=0, tiled=True)]
    unnamed x24 -> x15, local copies, waits for them, and re-layouts: 6.72 us -> 2.9 us
    unnamed x2 -> x1, other arithmetic: 2.22 us -> 0.02 us
    dot_general x1, matrix products: 1.11 us -> 2.94 us  [local(): jnp.dot(localize, all_products, precision=highest)]
    convert_element_type x3 -> x2, other arithmetic: 2.72 us -> 3.14 us  [the longest x1 3.1 us: local(): background_members.reshape(members, -1, lanes).astype(jnp.bfloat16)]
where the time goes in v3:
time: 89.3 us; the launch traced here: 88.8 us
  waiting for transfers between devices  29.1 us (33%)
  starting transfers between devices  21.9 us (25%)
  blocking collectives  17.6 us (20%)
  local copies, waits for them, and re-layouts  8.15 us (9%)
  other arithmetic  5.62 us (6%)
  matrix products  5.53 us (6%)
    all_to_all x1, blocking collectives, local(): lax.all_to_all(increment_low, 'slab', split_axis=0, concat_axis=0, tiled=...  17.6 us
    all_to_all x1, waiting for transfers between devices, local(): lax.all_to_all(copies, 'obs', split_axis=0, concat_axis=0, tiled=True)  17.5 us
    all_to_all x1, starting transfers between devices, local(): lax.all_to_all(work_low, 'slab', split_axis=0, concat_axis=0, tiled=True)  15 us
    all_to_all x1, waiting for transfers between devices, local(): lax.all_to_all(work_low, 'slab', split_axis=0, concat_axis=0, tiled=True)  11.6 us
    all_to_all x1, starting transfers between devices, local(): lax.all_to_all(copies, 'obs', split_axis=0, concat_axis=0, tiled=True)  6.95 us
    convert_element_type x1, other arithmetic, local(): background_members.reshape(members, -1, lanes).astype(jnp.bfloat16)  3.1 us
    gather x2, local copies, waits for them, and re-layouts, block_products(): prior_value = jnp.take(tile_work, positions, axis=1)  2.99 us
    dot_general x1, matrix products, local(): jnp.dot(localize, all_products, precision=highest)  2.94 us
  transfers between devices with their start and end apart: 2, of which 2 were waited for; matrix products, arithmetic and copies ran while one was open for 1% of the time, Pallas kernels for 0%

profile of v3, /device:TPU:1, one launch (start us, length us, event | category | flops | bytes accessed | tf_op | source)
XLA Modules:
  0.0 88.8 jit_solution(427141811857426849)
XLA Ops:
  0.0 3.1 %convert_reduce_fusion = bf16[131072]{0:T(1024)(128)(2,1)} fusion(f32[1,131072]{1,0:T(1,128)} %param.8), kind=kLoop, calls=%fused_computation.8 | loop fusion | flops 131072 | bytes 786432 | tf_op jit(solution)/shard_map/convert_element_type | solution.py:52
  3.1 0.0 copy-start.1
  3.1 15.0 %all-to-all-start = ((bf16[64,16,128]{2,1,0:T(8,128)(2,1)}), bf16[64,16,128]{2,1,0:T(8,128)(2,1)S(1)}, u32[]{:S(2)}, u32[]{:S(2)}) async-start(bf16[64,16,128]{2,1,0:T(8,128)(2,1)} %bitcast.25), calls=%async_computation | async-start | bytes 524288 | tf_op jit(solution)/shard_map/all_to_all | solution.py:53
  18.7 0.0 copy-done.1
  18.7 0.0 copy-start.2
  18.8 0.7 copy-done.2
  19.5 11.6 %all-to-all-done = bf16[64,16,128]{2,1,0:T(8,128)(2,1)S(1)} async-done(((bf16[64,16,128]{2,1,0:T(8,128)(2,1)}), bf16[64,16,128]{2,1,0:T(8,128)(2,1)S(1)}, u32[]{:S(2)}, u32[]{:S(2)}) %all-to-all-start) | async-done | bytes 262176 | tf_op jit(solution)/shard_map/all_to_all | solution.py:53
  31.1 0.3 copy.48
  31.4 2.8 %gather_fusion = f32[1024,64]{1,0:T(8,128)S(1)} fusion(f32[64,2048]{0,1:T(8,128)S(1)} %bitcast.43, s32[1024]{0:T(1024)S(1)} %broadcast_clamp_fusion), kind=kCustom, calls=%fused_computation | custom fusion | bytes 528384 | tf_op jit(solution)/shard_map/jit(_take)/gather | solution.py:23
  34.2 0.4 fusion.3
  34.6 0.5 multiply_reduce_fusion
  35.2 0.0 copy-start.3
  35.2 0.2 copy.44
  35.4 0.5 copy-done.3
  35.8 0.0 copy-start.6
  35.9 0.7 copy-done.6
  36.5 0.2 convolution_convert_fusion.1
  36.7 0.2 broadcast_in_dim.59
  36.9 0.8 broadcast_in_dim.60
  37.8 0.0 copy-start.5
  37.8 0.0 copy-start.4
  37.8 7.0 %all-to-all-start.1 = ((bf16[8,8,4096]{2,1,0:T(8,128)(2,1)}), bf16[8,8,4096]{2,1,0:T(8,128)(2,1)S(1)}, u32[]{:S(2)}, u32[]{:S(2)}) async-start(bf16[8,8,4096]{2,1,0:T(8,128)(2,1)} %broadcast_in_dim.60), calls=%async_computation.1 | async-start | bytes 1048576 | tf_op jit(solution)/shard_map/all_to_all | solution.py:69
  44.7 0.0 copy-done.5
  44.7 0.1 copy.41
  44.8 0.0 copy-done.4
  44.8 0.1 copy.40
  44.9 0.1 select_reduce_fusion
  45.0 0.1 convert_reduce_fusion.1
  45.1 0.1 div.45
  45.2 17.5 %all-to-all-done.1 = bf16[8,8,4096]{2,1,0:T(8,128)(2,1)S(1)} async-done(((bf16[8,8,4096]{2,1,0:T(8,128)(2,1)}), bf16[8,8,4096]{2,1,0:T(8,128)(2,1)S(1)}, u32[]{:S(2)}, u32[]{:S(2)}) %all-to-all-start.1) | async-done | bytes 524320 | tf_op jit(solution)/shard_map/all_to_all | solution.py:69
  62.7 0.5 copy.45
  63.2 2.9 %fusion.15 = f32[32,64,64]{2,0,1:T(8,128)S(1)} fusion(bf16[64,64,64]{2,1,0:T(8,128)(2,1)S(1)} %bitcast.46, f32[32,64]{1,0:T(8,128)S(1)} %select_reduce_fusion), kind=kOutput, calls=%fused_computation.27 | convolution fusion | flops 100663296 | bytes 1056768 | tf_op jit(solution)/shard_map/dot_general | solution.py:77
  66.1 2.4 %convolution_convert_fusion = bf16[32,64,64]{2,1,0:T(8,128)(2,1)S(1)} fusion(f32[32,64,64]{2,0,1:T(8,128)S(1)} %fusion.15, f32[64,32,64]{0,2,1:T(8,128)S(1)} %bitcast.44, f32[32,64]{1,0:T(8,128)S(1)} %div.45), kind=kOutput, calls=%fused_computation.1 | convolution fusion | flops 100925440 | bytes 1318912 | tf_op jit(solution)/shard_map/bmn,nbp->mbp/dot_general | solution.py:79
  68.5 0.3 copy.47
  68.8 17.6 %all_to_all.15 = bf16[64,16,128]{2,1,0:T(8,128)(2,1)S(1)} all-to-all(bf16[64,16,128]{2,1,0:T(8,128)(2,1)S(1)} %copy.47), channel_id=1, replica_groups=mesh['slab'=64,'obs'=8] {'slab'}, dimensions={0} | all-to-all | bytes 524288 | tf_op jit(solution)/shard_map/all_to_all | solution.py:81
  86.4 0.0 copy-start
  86.4 1.0 %copy-done = f32[1,131072]{1,0:T(1,128)S(1)} copy-done((f32[1,131072]{1,0:T(1,128)S(1)}, f32[1,131072]{1,0:T(1,128)}, u32[]{:S(2)}) %copy-start) | copy-done | bytes 524312
  87.4 1.3 %add.54 = f32[1,131072]{1,0:T(1,128)} add(f32[1,131072]{1,0:T(1,128)S(1)} %copy-done, f32[1,131072]{1,0:T(1,128)S(1)} %bitcast.49) | non-fusion elementwise | flops 131072 | bytes 1572864 | tf_op jit(solution)/shard_map/add | solution.py:82
  (12 shorter events, 0.2 us)
Async XLA Ops:
  3.1 15.6 %copy-start.1 = (bf16[64,1,1024]{2,0,1:T(8,128)(2,1)S(1)}, bf16[64,1,1024]{2,0,1:T(8,128)(2,1)}, u32[]{:S(2)}) copy-start(bf16[64,1,1024]{2,0,1:T(8,128)(2,1)} %param.9) | copy-start | bytes 393220
  3.1 28.0 %all-to-all-start = ((bf16[64,16,128]{2,1,0:T(8,128)(2,1)}), bf16[64,16,128]{2,1,0:T(8,128)(2,1)S(1)}, u32[]{:S(2)}, u32[]{:S(2)}) async-start(bf16[64,16,128]{2,1,0:T(8,128)(2,1)} %bitcast.25), calls=%async_computation | async-start | bytes 524288 | tf_op jit(solution)/shard_map/all_to_all | solution.py:53
  18.7 0.7 copy-start.2
  35.2 0.7 copy-start.3
  35.8 0.7 copy-start.6
  37.8 7.0 %copy-start.5 = (f32[1,32,8]{1,2,0:T(8,128)S(1)}, f32[1,32,8]{1,2,0:T(8,128)}, u32[]{:S(2)}) copy-start(f32[1,32,8]{1,2,0:T(8,128)} %param.15) | copy-start | bytes 3076
  37.8 7.0 %copy-start.4 = (s32[1,32,8]{1,2,0:T(8,128)S(1)}, s32[1,32,8]{1,2,0:T(8,128)}, u32[]{:S(2)}) copy-start(s32[1,32,8]{1,2,0:T(8,128)} %param.14) | copy-start | bytes 3076
  37.8 24.9 %all-to-all-start.1 = ((bf16[8,8,4096]{2,1,0:T(8,128)(2,1)}), bf16[8,8,4096]{2,1,0:T(8,128)(2,1)S(1)}, u32[]{:S(2)}, u32[]{:S(2)}) async-start(bf16[8,8,4096]{2,1,0:T(8,128)(2,1)} %broadcast_in_dim.60), calls=%async_computation.1 | async-start | bytes 1048576 | tf_op jit(solution)/shard_map/all_to_all | solution.py:69
  86.4 1.0 %copy-start = (f32[1,131072]{1,0:T(1,128)S(1)}, f32[1,131072]{1,0:T(1,128)}, u32[]{:S(2)}) copy-start(f32[1,131072]{1,0:T(1,128)} %param.8) | copy-start | bytes 1572868

commit v4 on v3

--- a/solution.py
+++ b/solution.py
@@ -49,9 +49,10 @@
 ):
     members = lax.axis_size("slab")
     lanes = 128
-    work_low = background_members.reshape(members, -1, lanes).astype(jnp.bfloat16)
-    tile_low = lax.all_to_all(work_low, "slab", split_axis=0, concat_axis=0, tiled=True)
-    tile_work = tile_low.reshape(members, -1).astype(jnp.float32)
+    pieces = background_members.reshape(members, -1, lanes)
+    tile = lax.all_to_all(pieces, "slab", split_axis=0, concat_axis=0, tiled=True)
+    tile_low = lax.optimization_barrier(tile.reshape(members, -1).astype(jnp.bfloat16))
+    tile_work = tile_low.astype(jnp.float32)
     blocks = coupling_listing.shape[1]
     deviation = tile_work - jnp.mean(tile_work, axis=0, keepdims=True)
 
@@ -74,9 +75,10 @@
     factor = taper_factors[0] / (members - 1)
     choose = block_links[..., None] == jnp.arange(obs_blocks, dtype=jnp.int32)
     localize = jnp.sum(jnp.where(choose, factor[..., None], jnp.float32(0.0)), axis=1)
-    ensemble = jnp.dot(localize, all_products, precision=highest).reshape(blocks, members, members)
+    ensemble = jnp.dot(localize, all_products, precision=lax.Precision.HIGH)
+    ensemble = ensemble.reshape(blocks, members, members)
     region_dev = deviation.reshape(members, blocks, -1)
-    increment = jnp.einsum("bmn,nbp->mbp", ensemble, region_dev, precision=highest)
+    increment = jnp.einsum("bmn,nbp->mbp", ensemble, region_dev, precision=lax.Precision.HIGH)
     increment_low = increment.reshape(members, -1, lanes).astype(jnp.bfloat16)
     back = lax.all_to_all(increment_low, "slab", split_axis=0, concat_axis=0, tiled=True)
     return background_members + back.reshape(background_members.shape).astype(jnp.float32)

time: 89.3 us -> 86.2 us (0.965)
  matrix products: 5.53 us -> 3.76 us
  waiting for transfers between devices: 29.1 us -> 27.5 us
  local copies, waits for them, and re-layouts: 8.15 us -> 9.36 us
    convert_element_type x1, other arithmetic: 3.1 us -> 0.07 us  [local(): tile_work = tile_low.astype(jnp.float32)]
    unnamed x1 -> x2, other arithmetic: 0.02 us -> 1.8 us
    dot_general x2, matrix products: 5.33 us -> 3.57 us  [the longest x1 2.02 us: local(): ensemble = jnp.dot(localize, all_products, precision=lax.Precision.HIGH)]
    all_to_all x1, waiting for transfers between devices: 11.6 us -> 10.2 us  [local(): lax.all_to_all(pieces, 'slab', split_axis=0, concat_axis=0, tiled=True)]
    unnamed x15, local copies, waits for them, and re-layouts: 2.9 us -> 4.12 us
where the time goes in v4:
time: 86.2 us; the launch traced here: 85.7 us
  waiting for transfers between devices  27.5 us (32%)
  starting transfers between devices  21.8 us (25%)
  blocking collectives  17.6 us (20%)
  local copies, waits for them, and re-layouts  9.36 us (11%)
  other arithmetic  4.85 us (6%)
  matrix products  3.76 us (4%)
    all_to_all x1, blocking collectives, local(): lax.all_to_all(increment_low, 'slab', split_axis=0, concat_axis=0, tiled=...  17.6 us
    all_to_all x1, waiting for transfers between devices, local(): lax.all_to_all(copies, 'obs', split_axis=0, concat_axis=0, tiled=True)  17.2 us
    all_to_all x1, starting transfers between devices, local(): lax.all_to_all(pieces, 'slab', split_axis=0, concat_axis=0, tiled=True)  15 us
    all_to_all x1, waiting for transfers between devices, local(): lax.all_to_all(pieces, 'slab', split_axis=0, concat_axis=0, tiled=True)  10.2 us
    all_to_all x1, starting transfers between devices, local(): lax.all_to_all(copies, 'obs', split_axis=0, concat_axis=0, tiled=True)  6.82 us
    unnamed x15, local copies, waits for them, and re-layouts  4.12 us
    gather x2, local copies, waits for them, and re-layouts, block_products(): prior_value = jnp.take(tile_work, positions, axis=1)  2.99 us
    dot_general x1, matrix products, local(): ensemble = jnp.dot(localize, all_products, precision=lax.Precision.HIGH)  2.02 us
  transfers between devices with their start and end apart: 2, of which 2 were waited for; matrix products, arithmetic and copies ran while one was open for 1% of the time, Pallas kernels for 0%

profile of v4, /device:TPU:1, one launch (start us, length us, event | category | flops | bytes accessed | tf_op | source)
XLA Modules:
  0.0 85.7 jit_solution(8889676896778407256)
XLA Ops:
  0.0 1.8 %convert.3 = bf16[64,16,128]{2,1,0:T(8,128)(2,1)} convert(f32[64,16,128]{2,1,0:T(8,128)} %bitcast.50) | non-fusion elementwise | flops 131072 | bytes 786432
  1.8 0.0 copy-start.1
  1.8 15.0 %all-to-all-start = ((bf16[64,16,128]{2,1,0:T(8,128)(2,1)}), bf16[64,16,128]{2,1,0:T(8,128)(2,1)S(1)}, u32[]{:S(2)}, u32[]{:S(2)}) async-start(bf16[64,16,128]{2,1,0:T(8,128)(2,1)} %convert.3), calls=%async_computation | async-start | bytes 524288 | tf_op jit(solution)/shard_map/all_to_all | solution.py:53
  17.4 0.0 copy-done.1
  17.4 0.0 copy-start.5
  17.4 0.7 copy-done.5
  18.1 0.0 copy-start.2
  18.1 0.7 copy-done.2
  18.8 0.0 copy-start.3
  18.9 0.1 copy.39
  18.9 0.5 copy-done.3
  19.5 0.1 copy.38
  19.6 10.2 %all-to-all-done = bf16[64,16,128]{2,1,0:T(8,128)(2,1)S(1)} async-done(((bf16[64,16,128]{2,1,0:T(8,128)(2,1)}), bf16[64,16,128]{2,1,0:T(8,128)(2,1)S(1)}, u32[]{:S(2)}, u32[]{:S(2)}) %all-to-all-start) | async-done | bytes 262176 | tf_op jit(solution)/shard_map/all_to_all | solution.py:53
  29.8 0.3 copy.37
  30.2 0.1 convert_element_type.53
  30.2 2.8 %gather_fusion = f32[1024,64]{1,0:T(8,128)S(1)} fusion(f32[64,2048]{0,1:T(8,128)S(1)} %convert_element_type.53, s32[1024]{0:T(1024)S(1)} %broadcast_clamp_fusion), kind=kCustom, calls=%fused_computation | custom fusion | bytes 528384 | tf_op jit(solution)/shard_map/jit(_take)/gather | solution.py:23
  33.1 0.4 fusion.1
  33.4 0.5 multiply_reduce_fusion
  34.0 0.0 copy-start.4
  34.0 0.2 copy.41
  34.2 0.5 copy-done.4
  34.6 0.0 copy-start.6
  34.7 0.7 copy-done.6
  35.3 0.2 convolution_convert_fusion.1
  35.5 0.2 broadcast_in_dim.59
  35.7 0.8 broadcast_in_dim.60
  36.6 6.8 %all-to-all-start.1 = ((bf16[8,8,4096]{2,1,0:T(8,128)(2,1)}), bf16[8,8,4096]{2,1,0:T(8,128)(2,1)S(1)}, u32[]{:S(2)}, u32[]{:S(2)}) async-start(bf16[8,8,4096]{2,1,0:T(8,128)(2,1)} %broadcast_in_dim.60), calls=%async_computation.1 | async-start | bytes 1048576 | tf_op jit(solution)/shard_map/all_to_all | solution.py:70
  43.4 0.1 select_reduce_fusion
  43.5 0.2 convert_reduce_fusion
  43.8 0.3 broadcast_subtract_fusion
  44.1 17.2 %all-to-all-done.1 = bf16[8,8,4096]{2,1,0:T(8,128)(2,1)S(1)} async-done(((bf16[8,8,4096]{2,1,0:T(8,128)(2,1)}), bf16[8,8,4096]{2,1,0:T(8,128)(2,1)S(1)}, u32[]{:S(2)}, u32[]{:S(2)}) %all-to-all-start.1) | async-done | bytes 524320 | tf_op jit(solution)/shard_map/all_to_all | solution.py:70
  61.3 0.5 copy.42
  61.8 2.0 %fusion.13 = f32[32,64,64]{2,0,1:T(8,128)S(1)} fusion(bf16[64,64,64]{2,1,0:T(8,128)(2,1)S(1)} %bitcast.49, f32[32,64]{1,0:T(8,128)S(1)} %select_reduce_fusion), kind=kOutput, calls=%fused_computation.25 | convolution fusion | flops 50331648 | bytes 1056768 | tf_op jit(solution)/shard_map/dot_general | solution.py:78
  63.8 1.5 %convolution_convert_fusion = bf16[32,64,64]{2,1,0:T(8,128)(2,1)S(1)} fusion(f32[64,32,64]{0,2,1:T(8,128)S(1)} %bitcast.48, f32[32,64,64]{2,0,1:T(8,128)S(1)} %fusion.13), kind=kOutput, calls=%fused_computation.1 | convolution fusion | flops 50462720 | bytes 1310720 | tf_op jit(solution)/shard_map/bmn,nbp->mbp/dot_general | solution.py:81
  65.4 0.3 copy.44
  65.7 17.6 %all_to_all.15 = bf16[64,16,128]{2,1,0:T(8,128)(2,1)S(1)} all-to-all(bf16[64,16,128]{2,1,0:T(8,128)(2,1)S(1)} %copy.44), channel_id=1, replica_groups=mesh['slab'=64,'obs'=8] {'slab'}, dimensions={0} | all-to-all | bytes 524288 | tf_op jit(solution)/shard_map/all_to_all | solution.py:83
  83.3 0.0 copy-start
  83.3 1.0 %copy-done = f32[1,131072]{1,0:T(1,128)S(1)} copy-done((f32[1,131072]{1,0:T(1,128)S(1)}, f32[1,131072]{1,0:T(1,128)}, u32[]{:S(2)}) %copy-start) | copy-done | bytes 524312
  84.3 1.3 %add.54 = f32[1,131072]{1,0:T(1,128)} add(f32[1,131072]{1,0:T(1,128)S(1)} %copy-done, f32[1,131072]{1,0:T(1,128)S(1)} %bitcast.53) | non-fusion elementwise | flops 131072 | bytes 1572864 | tf_op jit(solution)/shard_map/add | solution.py:84
  (12 shorter events, 0.2 us)
Async XLA Ops:
  1.8 15.6 %copy-start.1 = (bf16[64,1,1024]{2,0,1:T(8,128)(2,1)S(1)}, bf16[64,1,1024]{2,0,1:T(8,128)(2,1)}, u32[]{:S(2)}) copy-start(bf16[64,1,1024]{2,0,1:T(8,128)(2,1)} %param.9) | copy-start | bytes 393220
  1.8 28.0 %all-to-all-start = ((bf16[64,16,128]{2,1,0:T(8,128)(2,1)}), bf16[64,16,128]{2,1,0:T(8,128)(2,1)S(1)}, u32[]{:S(2)}, u32[]{:S(2)}) async-start(bf16[64,16,128]{2,1,0:T(8,128)(2,1)} %convert.3), calls=%async_computation | async-start | bytes 524288 | tf_op jit(solution)/shard_map/all_to_all | solution.py:53
  17.4 0.7 copy-start.5
  18.1 0.7 copy-start.2
  18.8 0.7 copy-start.3
  34.0 0.7 copy-start.4
  34.6 0.7 copy-start.6
  36.6 24.8 %all-to-all-start.1 = ((bf16[8,8,4096]{2,1,0:T(8,128)(2,1)}), bf16[8,8,4096]{2,1,0:T(8,128)(2,1)S(1)}, u32[]{:S(2)}, u32[]{:S(2)}) async-start(bf16[8,8,4096]{2,1,0:T(8,128)(2,1)} %broadcast_in_dim.60), calls=%async_computation.1 | async-start | bytes 1048576 | tf_op jit(solution)/shard_map/all_to_all | solution.py:70
  83.3 1.0 %copy-start = (f32[1,131072]{1,0:T(1,128)S(1)}, f32[1,131072]{1,0:T(1,128)}, u32[]{:S(2)}) copy-start(f32[1,131072]{1,0:T(1,128)} %param.8) | copy-start | bytes 1572868

commit v5 on v4

--- a/solution.py
+++ b/solution.py
@@ -10,23 +10,20 @@
 
 
 def block_products(
-    tile_work,
-    measurement_jitter,
-    measurement_readings,
+    tile_low,
+    observed,
     measurement_noise_spread,
     measurement_grid_location,
     active_tallies,
 ):
-    members = tile_work.shape[0]
+    members = tile_low.shape[0]
     positions = measurement_grid_location[0]
     obs_count = positions.shape[0]
-    prior_value = jnp.take(tile_work, positions, axis=1)
+    prior_value = jnp.take(tile_low, positions, axis=1).astype(jnp.float32)
     prior_shift = prior_value - jnp.mean(prior_value, axis=0, keepdims=True)
     spread = jnp.sum(prior_shift * prior_shift, axis=0, keepdims=True) / (members - 1)
     usable = jnp.arange(obs_count, dtype=jnp.int32)[None, :] < active_tallies[0, 0]
-    innovation = (
-        measurement_readings + measurement_jitter[:, 0, :].astype(jnp.float32) - prior_value
-    ) / (spread + measurement_noise_spread)
+    innovation = (observed - prior_value) / (spread + measurement_noise_spread)
     gain_input = jnp.where(usable, innovation, jnp.float32(0.0)).astype(jnp.bfloat16)
     prior_low = prior_shift.astype(jnp.bfloat16)
     return jnp.einsum(
@@ -51,16 +48,18 @@
     lanes = 128
     pieces = background_members.reshape(members, -1, lanes)
     tile = lax.all_to_all(pieces, "slab", split_axis=0, concat_axis=0, tiled=True)
-    tile_low = lax.optimization_barrier(tile.reshape(members, -1).astype(jnp.bfloat16))
+    observed = measurement_readings + measurement_jitter[:, 0, :].astype(jnp.float32)
+    tile_low, observed, noise = lax.optimization_barrier(
+        (tile.reshape(members, -1).astype(jnp.bfloat16), observed, measurement_noise_spread)
+    )
     tile_work = tile_low.astype(jnp.float32)
     blocks = coupling_listing.shape[1]
     deviation = tile_work - jnp.mean(tile_work, axis=0, keepdims=True)
 
     products = block_products(
-        tile_work,
-        measurement_jitter,
-        measurement_readings,
-        measurement_noise_spread,
+        tile_low,
+        observed,
+        noise,
         measurement_grid_location,
         active_tallies,
     )

time: 86.2 us -> 86.7 us (level)
  other arithmetic: 4.85 us -> 5.77 us
    unnamed x15, local copies, waits for them, and re-layouts: 4.12 us -> 3.03 us
    unnamed x2 -> x1, other arithmetic: 1.8 us -> 1.78 us
where the time goes in v5:
time: 86.7 us; the launch traced here: 86.2 us
  waiting for transfers between devices  27.7 us (32%)
  starting transfers between devices  21.8 us (25%)
  blocking collectives  17.6 us (20%)
  local copies, waits for them, and re-layouts  8.62 us (10%)
  other arithmetic  5.77 us (7%)
  matrix products  3.81 us (4%)
    all_to_all x1, blocking collectives, local(): lax.all_to_all(increment_low, 'slab', split_axis=0, concat_axis=0, tiled=...  17.6 us
    all_to_all x1, waiting for transfers between devices, local(): lax.all_to_all(copies, 'obs', split_axis=0, concat_axis=0, tiled=True)  17.2 us
    all_to_all x1, starting transfers between devices, local(): lax.all_to_all(pieces, 'slab', split_axis=0, concat_axis=0, tiled=True)  15 us
    all_to_all x1, waiting for transfers between devices, local(): lax.all_to_all(pieces, 'slab', split_axis=0, concat_axis=0, tiled=True)  10.5 us
    all_to_all x1, starting transfers between devices, local(): lax.all_to_all(copies, 'obs', split_axis=0, concat_axis=0, tiled=True)  6.82 us
    gather x2, local copies, waits for them, and re-layouts, block_products(): prior_value = jnp.take(tile_low, positions, axis=1).astype(jnp.float32)  3.35 us
    unnamed x15, local copies, waits for them, and re-layouts  3.03 us
    dot_general x1, matrix products, local(): ensemble = jnp.dot(localize, all_products, precision=lax.Precision.HIGH)  2.02 us
  transfers between devices with their start and end apart: 2, of which 2 were waited for; matrix products, arithmetic and copies ran while one was open for 1% of the time, Pallas kernels for 0%

profile of v5, /device:TPU:1, one launch (start us, length us, event | category | flops | bytes accessed | tf_op | source)
XLA Modules:
  0.0 86.2 jit_solution(5108096676190449408)
XLA Ops:
  0.0 1.8 %convert.5 = bf16[64,16,128]{2,1,0:T(8,128)(2,1)} convert(f32[64,16,128]{2,1,0:T(8,128)} %bitcast.52) | non-fusion elementwise | flops 131072 | bytes 786432
  1.8 0.0 copy-start.2
  1.8 0.0 copy-start.1
  1.8 15.0 %all-to-all-start = ((bf16[64,16,128]{2,1,0:T(8,128)(2,1)}), bf16[64,16,128]{2,1,0:T(8,128)(2,1)S(1)}, u32[]{:S(2)}, u32[]{:S(2)}) async-start(bf16[64,16,128]{2,1,0:T(8,128)(2,1)} %convert.5), calls=%async_computation | async-start | bytes 524288 | tf_op jit(solution)/shard_map/all_to_all | solution.py:50
  16.7 0.0 copy-done.2
  16.8 0.0 copy-start.6
  17.4 0.0 copy-done.6
  17.5 0.0 copy-done.1
  17.5 0.2 copy.42
  17.7 0.0 copy-start.4
  17.7 0.1 copy.44
  17.8 0.6 copy-done.4
  18.4 0.1 copy.43
  18.4 0.0 copy-start.3
  18.4 0.7 copy-done.3
  19.1 0.2 convert_add_fusion
  19.3 10.5 %all-to-all-done = bf16[64,16,128]{2,1,0:T(8,128)(2,1)S(1)} async-done(((bf16[64,16,128]{2,1,0:T(8,128)(2,1)}), bf16[64,16,128]{2,1,0:T(8,128)(2,1)S(1)}, u32[]{:S(2)}, u32[]{:S(2)}) %all-to-all-start) | async-done | bytes 262176 | tf_op jit(solution)/shard_map/all_to_all | solution.py:50
  29.8 0.3 copy.41
  30.2 3.2 %gather_fusion = bf16[1024,64]{1,0:T(8,128)(2,1)S(1)} fusion(bf16[64,2048]{0,1:T(8,128)(2,1)S(1)} %bitcast.46, s32[1024]{0:T(1024)S(1)} %broadcast_clamp_fusion), kind=kCustom, calls=%fused_computation | custom fusion | bytes 266240 | tf_op jit(solution)/shard_map/jit(_take)/gather | solution.py:22
  33.4 0.3 convert_reduce_fusion.1
  33.7 0.5 fusion.5
  34.2 0.0 copy-start.5
  34.2 0.1 copy.45
  34.4 0.5 copy-done.5
  34.9 0.9 %fusion.3 = bf16[64,1024]{0,1:T(8,128)(2,1)S(1)} fusion(f32[64,1024]{0,1:T(8,128)S(1)} %convert_add_fusion, f32[1024]{0:T(1024)S(1)} %bitcast.59, pred[1024]{0:T(1024)(128)(4,1)S(1)} %get-tuple-element.13, bf16[1024,64]{1,0:T(8,128)(2,1)S(1)} %gather_fusion, pred[1024]{0:T(1024)(128)(4,1)S(1)} %get-tuple-element.14), kind=kLoop, calls=%fused_computation.11 | loop fusion | flops 393216 | bytes 530432 | tf_op jit(solution)/shard_map/convert_element_type | solution.py:27
  35.8 0.2 convolution_convert_fusion.1
  36.0 0.2 broadcast_in_dim.59
  36.2 0.8 broadcast_in_dim.60
  37.1 6.8 %all-to-all-start.1 = ((bf16[8,8,4096]{2,1,0:T(8,128)(2,1)}), bf16[8,8,4096]{2,1,0:T(8,128)(2,1)S(1)}, u32[]{:S(2)}, u32[]{:S(2)}) async-start(bf16[8,8,4096]{2,1,0:T(8,128)(2,1)} %broadcast_in_dim.60), calls=%async_computation.1 | async-start | bytes 1048576 | tf_op jit(solution)/shard_map/all_to_all | solution.py:69
  43.9 0.1 select_reduce_fusion
  44.0 0.2 convert_reduce_fusion
  44.3 0.3 convert_subtract_fusion
  44.6 17.2 %all-to-all-done.1 = bf16[8,8,4096]{2,1,0:T(8,128)(2,1)S(1)} async-done(((bf16[8,8,4096]{2,1,0:T(8,128)(2,1)}), bf16[8,8,4096]{2,1,0:T(8,128)(2,1)S(1)}, u32[]{:S(2)}, u32[]{:S(2)}) %all-to-all-start.1) | async-done | bytes 524320 | tf_op jit(solution)/shard_map/all_to_all | solution.py:69
  61.8 0.5 copy.47
  62.3 2.0 %fusion.10 = f32[32,64,64]{2,0,1:T(8,128)S(1)} fusion(bf16[64,64,64]{2,1,0:T(8,128)(2,1)S(1)} %bitcast.51, f32[32,64]{1,0:T(8,128)S(1)} %select_reduce_fusion), kind=kOutput, calls=%fused_computation.24 | convolution fusion | flops 50331648 | bytes 1056768 | tf_op jit(solution)/shard_map/dot_general | solution.py:77
  64.3 1.5 %convolution_convert_fusion = bf16[32,64,64]{2,1,0:T(8,128)(2,1)S(1)} fusion(f32[64,32,64]{0,2,1:T(8,128)S(1)} %bitcast.50, f32[32,64,64]{2,0,1:T(8,128)S(1)} %fusion.10), kind=kOutput, calls=%fused_computation.3 | convolution fusion | flops 50462720 | bytes 1310720 | tf_op jit(solution)/shard_map/bmn,nbp->mbp/dot_general | solution.py:80
  65.9 0.3 copy.49
  66.2 17.6 %all_to_all.15 = bf16[64,16,128]{2,1,0:T(8,128)(2,1)S(1)} all-to-all(bf16[64,16,128]{2,1,0:T(8,128)(2,1)S(1)} %copy.49), channel_id=1, replica_groups=mesh['slab'=64,'obs'=8] {'slab'}, dimensions={0} | all-to-all | bytes 524288 | tf_op jit(solution)/shard_map/all_to_all | solution.py:82
  83.8 0.0 copy-start
  83.8 1.0 %copy-done = f32[1,131072]{1,0:T(1,128)S(1)} copy-done((f32[1,131072]{1,0:T(1,128)S(1)}, f32[1,131072]{1,0:T(1,128)}, u32[]{:S(2)}) %copy-start) | copy-done | bytes 524312
  84.8 1.3 %add.52 = f32[1,131072]{1,0:T(1,128)} add(f32[1,131072]{1,0:T(1,128)S(1)} %copy-done, f32[1,131072]{1,0:T(1,128)S(1)} %bitcast.55) | non-fusion elementwise | flops 131072 | bytes 1572864 | tf_op jit(solution)/shard_map/add | solution.py:83
  (10 shorter events, 0.1 us)
Async XLA Ops:
  1.8 15.0 %copy-start.2 = (s32[1,1024]{1,0:T(1,128)S(1)}, s32[1,1024]{1,0:T(1,128)}, u32[]{:S(2)}) copy-start(s32[1,1024]{1,0:T(1,128)} %param.12) | copy-start | bytes 12292
  1.8 15.7 %copy-start.1 = (bf16[64,1,1024]{2,0,1:T(8,128)(2,1)S(1)}, bf16[64,1,1024]{2,0,1:T(8,128)(2,1)}, u32[]{:S(2)}) copy-start(bf16[64,1,1024]{2,0,1:T(8,128)(2,1)} %param.9) | copy-start | bytes 393220
  1.8 28.0 %all-to-all-start = ((bf16[64,16,128]{2,1,0:T(8,128)(2,1)}), bf16[64,16,128]{2,1,0:T(8,128)(2,1)S(1)}, u32[]{:S(2)}, u32[]{:S(2)}) async-start(bf16[64,16,128]{2,1,0:T(8,128)(2,1)} %convert.5), calls=%async_computation | async-start | bytes 524288 | tf_op jit(solution)/shard_map/all_to_all | solution.py:50
  16.8 0.7 copy-start.6
  17.7 0.7 copy-start.4
  18.4 0.7 copy-start.3
  34.2 0.7 copy-start.5
  37.1 24.8 %all-to-all-start.1 = ((bf16[8,8,4096]{2,1,0:T(8,128)(2,1)}), bf16[8,8,4096]{2,1,0:T(8,128)(2,1)S(1)}, u32[]{:S(2)}, u32[]{:S(2)}) async-start(bf16[8,8,4096]{2,1,0:T(8,128)(2,1)} %broadcast_in_dim.60), calls=%async_computation.1 | async-start | bytes 1048576 | tf_op jit(solution)/shard_map/all_to_all | solution.py:69
  83.8 1.0 %copy-start = (f32[1,131072]{1,0:T(1,128)S(1)}, f32[1,131072]{1,0:T(1,128)}, u32[]{:S(2)}) copy-start(f32[1,131072]{1,0:T(1,128)} %param.8) | copy-start | bytes 1572868

commit v6 on v5

--- a/solution.py
+++ b/solution.py
@@ -10,16 +10,16 @@
 
 
 def block_products(
-    tile_low,
+    tile_work,
     observed,
     measurement_noise_spread,
     measurement_grid_location,
     active_tallies,
 ):
-    members = tile_low.shape[0]
+    members = tile_work.shape[0]
     positions = measurement_grid_location[0]
     obs_count = positions.shape[0]
-    prior_value = jnp.take(tile_low, positions, axis=1).astype(jnp.float32)
+    prior_value = jnp.take(tile_work, positions, axis=1)
     prior_shift = prior_value - jnp.mean(prior_value, axis=0, keepdims=True)
     spread = jnp.sum(prior_shift * prior_shift, axis=0, keepdims=True) / (members - 1)
     usable = jnp.arange(obs_count, dtype=jnp.int32)[None, :] < active_tallies[0, 0]
@@ -57,7 +57,7 @@
     deviation = tile_work - jnp.mean(tile_work, axis=0, keepdims=True)
 
     products = block_products(
-        tile_low,
+        tile_work,
         observed,
         noise,
         measurement_grid_location,

time: 86.7 us -> 86.4 us (level)
  no operation moved by 1% of the time
where the time goes in v6:
time: 86.4 us; the launch traced here: 85.9 us
  waiting for transfers between devices  27.7 us (32%)
  starting transfers between devices  21.8 us (25%)
  blocking collectives  17.6 us (20%)
  local copies, waits for them, and re-layouts  8.22 us (10%)
  other arithmetic  5.9 us (7%)
  matrix products  3.81 us (4%)
    all_to_all x1, blocking collectives, local(): lax.all_to_all(increment_low, 'slab', split_axis=0, concat_axis=0, tiled=...  17.6 us
    all_to_all x1, waiting for transfers between devices, local(): lax.all_to_all(copies, 'obs', split_axis=0, concat_axis=0, tiled=True)  17.2 us
    all_to_all x1, starting transfers between devices, local(): lax.all_to_all(pieces, 'slab', split_axis=0, concat_axis=0, tiled=True)  15 us
    all_to_all x1, waiting for transfers between devices, local(): lax.all_to_all(pieces, 'slab', split_axis=0, concat_axis=0, tiled=True)  10.5 us
    all_to_all x1, starting transfers between devices, local(): lax.all_to_all(copies, 'obs', split_axis=0, concat_axis=0, tiled=True)  6.82 us
    gather x2, local copies, waits for them, and re-layouts, block_products(): prior_value = jnp.take(tile_work, positions, axis=1)  2.99 us
    unnamed x15, local copies, waits for them, and re-layouts  2.98 us
    dot_general x1, matrix products, local(): ensemble = jnp.dot(localize, all_products, precision=lax.Precision.HIGH)  2.02 us
  transfers between devices with their start and end apart: 2, of which 2 were waited for; matrix products, arithmetic and copies ran while one was open for 1% of the time, Pallas kernels for 0%

profile of v6, /device:TPU:1, one launch (start us, length us, event | category | flops | bytes accessed | tf_op | source)
XLA Modules:
  0.0 85.9 jit_solution(6751126000403009)
XLA Ops:
  0.0 1.8 %convert.5 = bf16[64,16,128]{2,1,0:T(8,128)(2,1)} convert(f32[64,16,128]{2,1,0:T(8,128)} %bitcast.52) | non-fusion elementwise | flops 131072 | bytes 786432
  1.8 0.0 copy-start.2
  1.8 0.0 copy-start.1
  1.8 15.0 %all-to-all-start = ((bf16[64,16,128]{2,1,0:T(8,128)(2,1)}), bf16[64,16,128]{2,1,0:T(8,128)(2,1)S(1)}, u32[]{:S(2)}, u32[]{:S(2)}) async-start(bf16[64,16,128]{2,1,0:T(8,128)(2,1)} %convert.5), calls=%async_computation | async-start | bytes 524288 | tf_op jit(solution)/shard_map/all_to_all | solution.py:50
  16.7 0.0 copy-done.2
  16.8 0.0 copy-start.6
  17.4 0.0 copy-done.6
  17.5 0.0 copy-done.1
  17.5 0.2 copy.42
  17.7 0.0 copy-start.4
  17.7 0.1 copy.44
  17.8 0.6 copy-done.4
  18.4 0.1 copy.43
  18.4 0.0 copy-start.3
  18.4 0.7 copy-done.3
  19.1 0.2 convert_add_fusion
  19.3 10.5 %all-to-all-done = bf16[64,16,128]{2,1,0:T(8,128)(2,1)S(1)} async-done(((bf16[64,16,128]{2,1,0:T(8,128)(2,1)}), bf16[64,16,128]{2,1,0:T(8,128)(2,1)S(1)}, u32[]{:S(2)}, u32[]{:S(2)}) %all-to-all-start) | async-done | bytes 262176 | tf_op jit(solution)/shard_map/all_to_all | solution.py:50
  29.8 0.3 copy.41
  30.2 0.1 convert_element_type.53
  30.2 2.8 %gather_fusion = f32[1024,64]{1,0:T(8,128)S(1)} fusion(f32[64,2048]{0,1:T(8,128)S(1)} %convert_element_type.53, s32[1024]{0:T(1024)S(1)} %broadcast_clamp_fusion), kind=kCustom, calls=%fused_computation | custom fusion | bytes 528384 | tf_op jit(solution)/shard_map/jit(_take)/gather | solution.py:22
  33.1 0.4 fusion.1
  33.4 0.5 multiply_reduce_fusion
  34.0 0.0 copy-start.5
  34.0 0.2 copy.45
  34.2 0.5 copy-done.5
  34.7 0.9 %select_convert_fusion = bf16[64,1024]{0,1:T(8,128)(2,1)S(1)} fusion(f32[64,1024]{0,1:T(8,128)S(1)} %convert_add_fusion, f32[1024,64]{1,0:T(8,128)S(1)} %gather_fusion, f32[1024]{0:T(1024)S(1)} %bitcast.59, pred[1024]{0:T(1024)(128)(4,1)S(1)} %get-tuple-element.14, pred[1024]{0:T(1024)(128)(4,1)S(1)} %get-tuple-element.13), kind=kLoop, calls=%fused_computation.6 | loop fusion | flops 327680 | bytes 661504 | tf_op jit(solution)/shard_map/convert_element_type | solution.py:27
  35.5 0.2 convolution_convert_fusion.1
  35.8 0.2 broadcast_in_dim.59
  36.0 0.8 broadcast_in_dim.60
  36.8 6.8 %all-to-all-start.1 = ((bf16[8,8,4096]{2,1,0:T(8,128)(2,1)}), bf16[8,8,4096]{2,1,0:T(8,128)(2,1)S(1)}, u32[]{:S(2)}, u32[]{:S(2)}) async-start(bf16[8,8,4096]{2,1,0:T(8,128)(2,1)} %broadcast_in_dim.60), calls=%async_computation.1 | async-start | bytes 1048576 | tf_op jit(solution)/shard_map/all_to_all | solution.py:69
  43.6 0.1 select_reduce_fusion
  43.8 0.2 convert_reduce_fusion
  44.0 0.3 broadcast_subtract_fusion
  44.3 17.2 %all-to-all-done.1 = bf16[8,8,4096]{2,1,0:T(8,128)(2,1)S(1)} async-done(((bf16[8,8,4096]{2,1,0:T(8,128)(2,1)}), bf16[8,8,4096]{2,1,0:T(8,128)(2,1)S(1)}, u32[]{:S(2)}, u32[]{:S(2)}) %all-to-all-start.1) | async-done | bytes 524320 | tf_op jit(solution)/shard_map/all_to_all | solution.py:69
  61.6 0.5 copy.47
  62.1 2.0 %fusion.5 = f32[32,64,64]{2,0,1:T(8,128)S(1)} fusion(bf16[64,64,64]{2,1,0:T(8,128)(2,1)S(1)} %bitcast.51, f32[32,64]{1,0:T(8,128)S(1)} %select_reduce_fusion), kind=kOutput, calls=%fused_computation.18 | convolution fusion | flops 50331648 | bytes 1056768 | tf_op jit(solution)/shard_map/dot_general | solution.py:77
  64.1 1.5 %convolution_convert_fusion = bf16[32,64,64]{2,1,0:T(8,128)(2,1)S(1)} fusion(f32[64,32,64]{0,2,1:T(8,128)S(1)} %bitcast.50, f32[32,64,64]{2,0,1:T(8,128)S(1)} %fusion.5), kind=kOutput, calls=%fused_computation.1 | convolution fusion | flops 50462720 | bytes 1310720 | tf_op jit(solution)/shard_map/bmn,nbp->mbp/dot_general | solution.py:80
  65.6 0.3 copy.49
  65.9 17.6 %all_to_all.15 = bf16[64,16,128]{2,1,0:T(8,128)(2,1)S(1)} all-to-all(bf16[64,16,128]{2,1,0:T(8,128)(2,1)S(1)} %copy.49), channel_id=1, replica_groups=mesh['slab'=64,'obs'=8] {'slab'}, dimensions={0} | all-to-all | bytes 524288 | tf_op jit(solution)/shard_map/all_to_all | solution.py:82
  83.5 0.0 copy-start
  83.6 1.0 %copy-done = f32[1,131072]{1,0:T(1,128)S(1)} copy-done((f32[1,131072]{1,0:T(1,128)S(1)}, f32[1,131072]{1,0:T(1,128)}, u32[]{:S(2)}) %copy-start) | copy-done | bytes 524312
  84.6 1.3 %add.52 = f32[1,131072]{1,0:T(1,128)} add(f32[1,131072]{1,0:T(1,128)S(1)} %copy-done, f32[1,131072]{1,0:T(1,128)S(1)} %bitcast.55) | non-fusion elementwise | flops 131072 | bytes 1572864 | tf_op jit(solution)/shard_map/add | solution.py:83
  (10 shorter events, 0.1 us)
Async XLA Ops:
  1.8 15.0 %copy-start.2 = (s32[1,1024]{1,0:T(1,128)S(1)}, s32[1,1024]{1,0:T(1,128)}, u32[]{:S(2)}) copy-start(s32[1,1024]{1,0:T(1,128)} %param.12) | copy-start | bytes 12292
  1.8 15.7 %copy-start.1 = (bf16[64,1,1024]{2,0,1:T(8,128)(2,1)S(1)}, bf16[64,1,1024]{2,0,1:T(8,128)(2,1)}, u32[]{:S(2)}) copy-start(bf16[64,1,1024]{2,0,1:T(8,128)(2,1)} %param.9) | copy-start | bytes 393220
  1.8 28.0 %all-to-all-start = ((bf16[64,16,128]{2,1,0:T(8,128)(2,1)}), bf16[64,16,128]{2,1,0:T(8,128)(2,1)S(1)}, u32[]{:S(2)}, u32[]{:S(2)}) async-start(bf16[64,16,128]{2,1,0:T(8,128)(2,1)} %convert.5), calls=%async_computation | async-start | bytes 524288 | tf_op jit(solution)/shard_map/all_to_all | solution.py:50
  16.8 0.7 copy-start.6
  17.7 0.7 copy-start.4
  18.4 0.7 copy-start.3
  34.0 0.7 copy-start.5
  36.8 24.8 %all-to-all-start.1 = ((bf16[8,8,4096]{2,1,0:T(8,128)(2,1)}), bf16[8,8,4096]{2,1,0:T(8,128)(2,1)S(1)}, u32[]{:S(2)}, u32[]{:S(2)}) async-start(bf16[8,8,4096]{2,1,0:T(8,128)(2,1)} %broadcast_in_dim.60), calls=%async_computation.1 | async-start | bytes 1048576 | tf_op jit(solution)/shard_map/all_to_all | solution.py:69
  83.5 1.0 %copy-start = (f32[1,131072]{1,0:T(1,128)S(1)}, f32[1,131072]{1,0:T(1,128)}, u32[]{:S(2)}) copy-start(f32[1,131072]{1,0:T(1,128)} %param.8) | copy-start | bytes 1572868

commit v7 on v4

--- a/solution.py
+++ b/solution.py
@@ -10,6 +10,7 @@
 
 
 def block_products(
+    tile_low,
     tile_work,
     measurement_jitter,
     measurement_readings,
@@ -20,7 +21,9 @@
     members = tile_work.shape[0]
     positions = measurement_grid_location[0]
     obs_count = positions.shape[0]
-    prior_value = jnp.take(tile_work, positions, axis=1)
+    points = tile_work.shape[1]
+    pick = (jnp.arange(points, dtype=jnp.int32)[:, None] == positions[None, :]).astype(jnp.bfloat16)
+    prior_value = jnp.dot(tile_low, pick, preferred_element_type=jnp.float32)
     prior_shift = prior_value - jnp.mean(prior_value, axis=0, keepdims=True)
     spread = jnp.sum(prior_shift * prior_shift, axis=0, keepdims=True) / (members - 1)
     usable = jnp.arange(obs_count, dtype=jnp.int32)[None, :] < active_tallies[0, 0]
@@ -57,6 +60,7 @@
     deviation = tile_work - jnp.mean(tile_work, axis=0, keepdims=True)
 
     products = block_products(
+        tile_low,
         tile_work,
         measurement_jitter,
         measurement_readings,

time: 86.2 us -> 81.1 us (0.941)
  local copies, waits for them, and re-layouts: 9.36 us -> 2.29 us
  waiting for transfers between devices: 27.5 us -> 29.2 us
  matrix products: 3.76 us -> 5.22 us
  other arithmetic: 4.85 us -> 3.96 us
    unnamed x15, local copies, waits for them, and re-layouts: 4.12 us -> 0.11 us
    gather x2 -> x0, local copies, waits for them, and re-layouts: 2.99 us -> none  [block_products(): prior_value = jnp.take(tile_work, positions, axis=1)]
    all_to_all x1, waiting for transfers between devices: 10.2 us -> 12.2 us  [local(): lax.all_to_all(pieces, 'slab', split_axis=0, concat_axis=0, tiled=True)]
    dot_general x0 -> x1, matrix products: none -> 1.46 us  [block_products(): prior_value = jnp.dot(tile_low, pick, preferred_element_type=jnp.float32)]
    unnamed x2 -> x1, other arithmetic: 1.8 us -> 1.82 us
where the time goes in v7:
time: 81.1 us; the launch traced here: 80.8 us
  waiting for transfers between devices  29.2 us (36%)
  starting transfers between devices  21.6 us (27%)
  blocking collectives  17.6 us (22%)
  matrix products  5.22 us (6%)
  other arithmetic  3.96 us (5%)
  local copies, waits for them, and re-layouts  2.29 us (3%)
  between operations  0.86 us (1%)
    all_to_all x1, blocking collectives, local(): lax.all_to_all(increment_low, 'slab', split_axis=0, concat_axis=0, tiled=...  17.6 us
    all_to_all x1, waiting for transfers between devices, local(): lax.all_to_all(copies, 'obs', split_axis=0, concat_axis=0, tiled=True)  17 us
    all_to_all x1, starting transfers between devices, local(): lax.all_to_all(pieces, 'slab', split_axis=0, concat_axis=0, tiled=True)  14.8 us
    all_to_all x1, waiting for transfers between devices, local(): lax.all_to_all(pieces, 'slab', split_axis=0, concat_axis=0, tiled=True)  12.2 us
    all_to_all x1, starting transfers between devices, local(): lax.all_to_all(copies, 'obs', split_axis=0, concat_axis=0, tiled=True)  6.82 us
    dot_general x1, matrix products, local(): ensemble = jnp.dot(localize, all_products, precision=lax.Precision.HIGH)  2.02 us
    unnamed x1, other arithmetic  1.82 us
  transfers between devices with their start and end apart: 2, of which 2 were waited for; matrix products, arithmetic and copies ran while one was open for 1% of the time, Pallas kernels for 0%

profile of v7, /device:TPU:1, one launch (start us, length us, event | category | flops | bytes accessed | tf_op | source)
XLA Modules:
  0.0 80.8 jit_solution(8901942539804321687)
XLA Ops:
  0.0 0.0 copy-start.3
  0.0 0.0 copy-start.1
  0.0 0.0 copy-start.5
  0.0 1.8 %convert.14 = bf16[64,16,128]{2,1,0:T(8,128)(2,1)} convert(f32[64,16,128]{2,1,0:T(8,128)} %bitcast.65) | non-fusion elementwise | flops 131072 | bytes 786432
  1.8 14.8 %all-to-all-start = ((bf16[64,16,128]{2,1,0:T(8,128)(2,1)}), bf16[64,16,128]{2,1,0:T(8,128)(2,1)S(1)}, u32[]{:S(2)}, u32[]{:S(2)}) async-start(bf16[64,16,128]{2,1,0:T(8,128)(2,1)} %convert.14), calls=%async_computation | async-start | bytes 524288 | tf_op jit(solution)/shard_map/all_to_all | solution.py:56
  17.3 0.0 copy-done.3
  17.3 0.1 copy.31
  17.4 0.0 copy-done.1
  17.4 0.1 copy.30
  17.5 12.2 %all-to-all-done = bf16[64,16,128]{2,1,0:T(8,128)(2,1)S(1)} async-done(((bf16[64,16,128]{2,1,0:T(8,128)(2,1)}), bf16[64,16,128]{2,1,0:T(8,128)(2,1)S(1)}, u32[]{:S(2)}, u32[]{:S(2)}) %all-to-all-start) | async-done | bytes 262176 | tf_op jit(solution)/shard_map/all_to_all | solution.py:56
  29.7 0.1 copy.51
  29.8 0.0 copy-done.5
  29.8 0.0 copy-start.2
  29.8 0.0 copy-start.4
  29.8 0.0 copy-start.6
  29.9 1.5 %fusion.16 = (f32[1024]{0:T(1024)S(1)}, f32[1024,64]{0,1:T(8,128)S(1)}) fusion(bf16[64,2048]{1,0:T(8,128)(2,1)S(1)} %bitcast.69, s32[1024]{0:T(1024)S(1)} %bitcast.75), kind=kOutput, calls=%fused_computation.32 | convolution fusion | flops 270597120 | bytes 532480 | tf_op jit(solution)/shard_map/dot_general | solution.py:26
  31.3 0.1 multiply_reduce_fusion
  31.4 0.0 copy-done.2
  31.4 0.0 copy-done.4
  31.4 0.0 copy-done.6
  31.4 0.2 convolution_convert_fusion.1
  31.7 0.2 broadcast_in_dim.42
  31.8 0.8 %broadcast_in_dim.43 = bf16[8,8,4096]{2,1,0:T(8,128)(2,1)} broadcast(bf16[8,4096]{1,0:T(8,128)(2,1)S(1)} %broadcast_in_dim.42), dimensions={1,2} | broadcast | bytes 589824 | tf_op jit(solution)/shard_map/broadcast_in_dim | solution.py:73
  32.7 6.8 %all-to-all-start.1 = ((bf16[8,8,4096]{2,1,0:T(8,128)(2,1)}), bf16[8,8,4096]{2,1,0:T(8,128)(2,1)S(1)}, u32[]{:S(2)}, u32[]{:S(2)}) async-start(bf16[8,8,4096]{2,1,0:T(8,128)(2,1)} %broadcast_in_dim.43), calls=%async_computation.1 | async-start | bytes 1048576 | tf_op jit(solution)/shard_map/all_to_all | solution.py:74
  39.5 0.1 select_reduce_fusion
  39.6 0.3 copy.29
  39.9 0.2 convert_reduce_fusion
  40.1 0.3 convert_subtract_fusion
  40.5 17.0 %all-to-all-done.1 = bf16[8,8,4096]{2,1,0:T(8,128)(2,1)S(1)} async-done(((bf16[8,8,4096]{2,1,0:T(8,128)(2,1)}), bf16[8,8,4096]{2,1,0:T(8,128)(2,1)S(1)}, u32[]{:S(2)}, u32[]{:S(2)}) %all-to-all-start.1) | async-done | bytes 524320 | tf_op jit(solution)/shard_map/all_to_all | solution.py:74
  57.4 0.5 copy.34
  57.9 2.0 %fusion.14 = f32[32,64,64]{2,0,1:T(8,128)S(1)} fusion(bf16[64,64,64]{2,1,0:T(8,128)(2,1)S(1)} %bitcast.64, f32[32,64]{1,0:T(8,128)S(1)} %select_reduce_fusion), kind=kOutput, calls=%fused_computation.25 | convolution fusion | flops 50331648 | bytes 1056768 | tf_op jit(solution)/shard_map/dot_general | solution.py:82
  60.0 1.5 %convolution_convert_fusion = bf16[32,64,64]{2,1,0:T(8,128)(2,1)S(1)} fusion(f32[64,32,64]{0,2,1:T(8,128)S(1)} %bitcast.63, f32[32,64,64]{2,0,1:T(8,128)S(1)} %fusion.14), kind=kOutput, calls=%fused_computation.5 | convolution fusion | flops 50462720 | bytes 1310720 | tf_op jit(solution)/shard_map/bmn,nbp->mbp/dot_general | solution.py:85
  61.5 0.0 copy-start
  61.5 0.3 copy.36
  61.8 17.6 %all_to_all.15 = bf16[64,16,128]{2,1,0:T(8,128)(2,1)S(1)} all-to-all(bf16[64,16,128]{2,1,0:T(8,128)(2,1)S(1)} %copy.36), channel_id=1, replica_groups=mesh['slab'=64,'obs'=8] {'slab'}, dimensions={0} | all-to-all | bytes 524288 | tf_op jit(solution)/shard_map/all_to_all | solution.py:87
  79.4 0.0 copy-done
  79.4 1.3 %add.20 = f32[1,131072]{1,0:T(1,128)} add(f32[1,131072]{1,0:T(1,128)S(1)} %copy-done, f32[1,131072]{1,0:T(1,128)S(1)} %bitcast.68) | non-fusion elementwise | flops 131072 | bytes 1572864 | tf_op jit(solution)/shard_map/add | solution.py:88
  (7 shorter events, 0.1 us)
Async XLA Ops:
  0.0 17.3 %copy-start.3 = (f32[1,32,8]{1,2,0:T(8,128)S(1)}, f32[1,32,8]{1,2,0:T(8,128)}, u32[]{:S(2)}) copy-start(f32[1,32,8]{1,2,0:T(8,128)} %param.15) | copy-start | bytes 3076
  0.0 17.4 %copy-start.1 = (s32[1,32,8]{1,2,0:T(8,128)S(1)}, s32[1,32,8]{1,2,0:T(8,128)}, u32[]{:S(2)}) copy-start(s32[1,32,8]{1,2,0:T(8,128)} %param.14) | copy-start | bytes 3076
  0.0 29.8 %copy-start.5 = (s32[1,1024]{1,0:T(1,128)S(1)}, s32[1,1024]{1,0:T(1,128)}, u32[]{:S(2)}) copy-start(s32[1,1024]{1,0:T(1,128)} %param.12) | copy-start | bytes 12292
  1.8 27.9 %all-to-all-start = ((bf16[64,16,128]{2,1,0:T(8,128)(2,1)}), bf16[64,16,128]{2,1,0:T(8,128)(2,1)S(1)}, u32[]{:S(2)}, u32[]{:S(2)}) async-start(bf16[64,16,128]{2,1,0:T(8,128)(2,1)} %convert.14), calls=%async_computation | async-start | bytes 524288 | tf_op jit(solution)/shard_map/all_to_all | solution.py:56
  29.8 1.6 %copy-start.2 = (f32[1,1024]{1,0:T(1,128)S(1)}, f32[1,1024]{1,0:T(1,128)}, u32[]{:S(2)}) copy-start(f32[1,1024]{1,0:T(1,128)} %param.11) | copy-start | bytes 12292
  29.8 1.6 %copy-start.4 = (bf16[64,1,1024]{2,0,1:T(8,128)(2,1)S(1)}, bf16[64,1,1024]{2,0,1:T(8,128)(2,1)}, u32[]{:S(2)}) copy-start(bf16[64,1,1024]{2,0,1:T(8,128)(2,1)} %param.9) | copy-start | bytes 393220
  29.8 1.6 %copy-start.6 = (f32[1,1024]{1,0:T(1,128)S(1)}, f32[1,1024]{1,0:T(1,128)}, u32[]{:S(2)}) copy-start(f32[1,1024]{1,0:T(1,128)} %param.10) | copy-start | bytes 12292
  32.7 24.8 %all-to-all-start.1 = ((bf16[8,8,4096]{2,1,0:T(8,128)(2,1)}), bf16[8,8,4096]{2,1,0:T(8,128)(2,1)S(1)}, u32[]{:S(2)}, u32[]{:S(2)}) async-start(bf16[8,8,4096]{2,1,0:T(8,128)(2,1)} %broadcast_in_dim.43), calls=%async_computation.1 | async-start | bytes 1048576 | tf_op jit(solution)/shard_map/all_to_all | solution.py:74
  61.5 17.9 %copy-start = (f32[1,131072]{1,0:T(1,128)S(1)}, f32[1,131072]{1,0:T(1,128)}, u32[]{:S(2)}) copy-start(f32[1,131072]{1,0:T(1,128)} %param.8) | copy-start | bytes 1572868

commit v8 on v7

--- a/solution.py
+++ b/solution.py
@@ -72,14 +72,18 @@
     flat = products.astype(jnp.bfloat16).reshape(products.shape[0], -1)
     copies = jnp.broadcast_to(flat[None], (groups,) + flat.shape)
     all_products = lax.all_to_all(copies, "obs", split_axis=0, concat_axis=0, tiled=True)
-    all_products = all_products.reshape(-1, flat.shape[1]).astype(jnp.float32)
+    all_products = all_products.reshape(-1, flat.shape[1])
     obs_blocks = all_products.shape[0]
 
     block_links = coupling_listing[0]
     factor = taper_factors[0] / (members - 1)
     choose = block_links[..., None] == jnp.arange(obs_blocks, dtype=jnp.int32)
     localize = jnp.sum(jnp.where(choose, factor[..., None], jnp.float32(0.0)), axis=1)
-    ensemble = jnp.dot(localize, all_products, precision=lax.Precision.HIGH)
+    localize_high = localize.astype(jnp.bfloat16)
+    localize_low = (localize - localize_high.astype(jnp.float32)).astype(jnp.bfloat16)
+    ensemble = jnp.dot(localize_high, all_products, preferred_element_type=jnp.float32) + jnp.dot(
+        localize_low, all_products, preferred_element_type=jnp.float32
+    )
     ensemble = ensemble.reshape(blocks, members, members)
     region_dev = deviation.reshape(members, blocks, -1)
     increment = jnp.einsum("bmn,nbp->mbp", ensemble, region_dev, precision=lax.Precision.HIGH)

time: 81.1 us -> 78.8 us (0.972)
  matrix products: 5.22 us -> 3.04 us
    dot_general x1 -> x2, matrix products: 2.02 us -> 0.43 us  [the longest x1 0.22 us: local(): jnp.dot(localize_low, all_products, preferred_element_type=jnp.float32)]
where the time goes in v8:
time: 78.8 us; the launch traced here: 78.5 us
  waiting for transfers between devices  29.2 us (37%)
  starting transfers between devices  21.6 us (27%)
  blocking collectives  17.6 us (22%)
  other arithmetic  3.96 us (5%)
  matrix products  3.04 us (4%)
  local copies, waits for them, and re-layouts  2.23 us (3%)
  between operations  0.86 us (1%)
    all_to_all x1, blocking collectives, local(): lax.all_to_all(increment_low, 'slab', split_axis=0, concat_axis=0, tiled=...  17.6 us
    all_to_all x1, waiting for transfers between devices, local(): lax.all_to_all(copies, 'obs', split_axis=0, concat_axis=0, tiled=True)  17 us
    all_to_all x1, starting transfers between devices, local(): lax.all_to_all(pieces, 'slab', split_axis=0, concat_axis=0, tiled=True)  14.8 us
    all_to_all x1, waiting for transfers between devices, local(): lax.all_to_all(pieces, 'slab', split_axis=0, concat_axis=0, tiled=True)  12.2 us
    all_to_all x1, starting transfers between devices, local(): lax.all_to_all(copies, 'obs', split_axis=0, concat_axis=0, tiled=True)  6.82 us
    unnamed x1, other arithmetic  1.82 us
  transfers between devices with their start and end apart: 2, of which 2 were waited for; matrix products, arithmetic and copies ran while one was open for 1% of the time, Pallas kernels for 0%

profile of v8, /device:TPU:1, one launch (start us, length us, event | category | flops | bytes accessed | tf_op | source)
XLA Modules:
  0.0 78.5 jit_solution(1453285174586353551)
XLA Ops:
  0.0 0.0 copy-start.3
  0.0 0.0 copy-start.1
  0.0 0.0 copy-start.5
  0.0 1.8 %convert.14 = bf16[64,16,128]{2,1,0:T(8,128)(2,1)} convert(f32[64,16,128]{2,1,0:T(8,128)} %bitcast.62) | non-fusion elementwise | flops 131072 | bytes 786432
  1.8 14.8 %all-to-all-start = ((bf16[64,16,128]{2,1,0:T(8,128)(2,1)}), bf16[64,16,128]{2,1,0:T(8,128)(2,1)S(1)}, u32[]{:S(2)}, u32[]{:S(2)}) async-start(bf16[64,16,128]{2,1,0:T(8,128)(2,1)} %convert.14), calls=%async_computation | async-start | bytes 524288 | tf_op jit(solution)/shard_map/all_to_all | solution.py:56
  17.3 0.0 copy-done.3
  17.3 0.1 copy.23
  17.4 0.0 copy-done.1
  17.4 0.1 copy.22
  17.5 12.2 %all-to-all-done = bf16[64,16,128]{2,1,0:T(8,128)(2,1)S(1)} async-done(((bf16[64,16,128]{2,1,0:T(8,128)(2,1)}), bf16[64,16,128]{2,1,0:T(8,128)(2,1)S(1)}, u32[]{:S(2)}, u32[]{:S(2)}) %all-to-all-start) | async-done | bytes 262176 | tf_op jit(solution)/shard_map/all_to_all | solution.py:56
  29.7 0.1 copy.39
  29.8 0.0 copy-done.5
  29.8 0.0 copy-start.2
  29.8 0.0 copy-start.4
  29.8 0.0 copy-start.6
  29.9 1.5 %fusion.18 = (f32[1024]{0:T(1024)S(1)}, f32[1024,64]{0,1:T(8,128)S(1)}) fusion(bf16[64,2048]{1,0:T(8,128)(2,1)S(1)} %bitcast.65, s32[1024]{0:T(1024)S(1)} %bitcast.71), kind=kOutput, calls=%fused_computation.36 | convolution fusion | flops 270597120 | bytes 532480 | tf_op jit(solution)/shard_map/dot_general | solution.py:26
  31.3 0.1 multiply_reduce_fusion
  31.4 0.0 copy-done.2
  31.4 0.0 copy-done.4
  31.4 0.0 copy-done.6
  31.4 0.2 convolution_convert_fusion.1
  31.7 0.2 broadcast_in_dim.42
  31.8 0.8 %broadcast_in_dim.43 = bf16[8,8,4096]{2,1,0:T(8,128)(2,1)} broadcast(bf16[8,4096]{1,0:T(8,128)(2,1)S(1)} %broadcast_in_dim.42), dimensions={1,2} | broadcast | bytes 589824 | tf_op jit(solution)/shard_map/broadcast_in_dim | solution.py:73
  32.7 6.8 %all-to-all-start.1 = ((bf16[8,8,4096]{2,1,0:T(8,128)(2,1)}), bf16[8,8,4096]{2,1,0:T(8,128)(2,1)S(1)}, u32[]{:S(2)}, u32[]{:S(2)}) async-start(bf16[8,8,4096]{2,1,0:T(8,128)(2,1)} %broadcast_in_dim.43), calls=%async_computation.1 | async-start | bytes 1048576 | tf_op jit(solution)/shard_map/all_to_all | solution.py:74
  39.5 0.1 select_reduce_fusion
  39.6 0.3 copy.21
  39.9 0.2 convert_reduce_fusion
  40.1 0.3 convert_subtract_fusion
  40.5 17.0 %all-to-all-done.1 = bf16[8,8,4096]{2,1,0:T(8,128)(2,1)S(1)} async-done(((bf16[8,8,4096]{2,1,0:T(8,128)(2,1)}), bf16[8,8,4096]{2,1,0:T(8,128)(2,1)S(1)}, u32[]{:S(2)}, u32[]{:S(2)}) %all-to-all-start.1) | async-done | bytes 524320 | tf_op jit(solution)/shard_map/all_to_all | solution.py:74
  57.4 0.2 fusion.3
  57.7 0.2 convolution_add_fusion
  57.9 0.4 reshape.76
  58.3 1.0 %convolution_convert_fusion = bf16[32,64,64]{2,1,0:T(8,128)(2,1)S(1)} fusion(f32[64,32,64]{0,2,1:T(8,128)S(1)} %bitcast.61, f32[32,64,64]{2,1,0:T(8,128)S(1)} %reshape.76), kind=kOutput, calls=%fused_computation.6 | convolution fusion | flops 50462720 | bytes 1310720 | tf_op jit(solution)/shard_map/bmn,nbp->mbp/dot_general | solution.py:89
  59.3 0.0 copy-start
  59.3 0.3 copy.26
  59.6 17.6 %all_to_all.15 = bf16[64,16,128]{2,1,0:T(8,128)(2,1)S(1)} all-to-all(bf16[64,16,128]{2,1,0:T(8,128)(2,1)S(1)} %copy.26), channel_id=1, replica_groups=mesh['slab'=64,'obs'=8] {'slab'}, dimensions={0} | all-to-all | bytes 524288 | tf_op jit(solution)/shard_map/all_to_all | solution.py:91
  77.2 0.0 copy-done
  77.2 1.3 %add.24 = f32[1,131072]{1,0:T(1,128)} add(f32[1,131072]{1,0:T(1,128)S(1)} %copy-done, f32[1,131072]{1,0:T(1,128)S(1)} %bitcast.64) | non-fusion elementwise | flops 131072 | bytes 1572864 | tf_op jit(solution)/shard_map/add | solution.py:92
  (7 shorter events, 0.1 us)
Async XLA Ops:
  0.0 17.3 %copy-start.3 = (f32[1,32,8]{1,2,0:T(8,128)S(1)}, f32[1,32,8]{1,2,0:T(8,128)}, u32[]{:S(2)}) copy-start(f32[1,32,8]{1,2,0:T(8,128)} %param.15) | copy-start | bytes 3076
  0.0 17.4 %copy-start.1 = (s32[1,32,8]{1,2,0:T(8,128)S(1)}, s32[1,32,8]{1,2,0:T(8,128)}, u32[]{:S(2)}) copy-start(s32[1,32,8]{1,2,0:T(8,128)} %param.14) | copy-start | bytes 3076
  0.0 29.8 %copy-start.5 = (s32[1,1024]{1,0:T(1,128)S(1)}, s32[1,1024]{1,0:T(1,128)}, u32[]{:S(2)}) copy-start(s32[1,1024]{1,0:T(1,128)} %param.12) | copy-start | bytes 12292
  1.8 27.9 %all-to-all-start = ((bf16[64,16,128]{2,1,0:T(8,128)(2,1)}), bf16[64,16,128]{2,1,0:T(8,128)(2,1)S(1)}, u32[]{:S(2)}, u32[]{:S(2)}) async-start(bf16[64,16,128]{2,1,0:T(8,128)(2,1)} %convert.14), calls=%async_computation | async-start | bytes 524288 | tf_op jit(solution)/shard_map/all_to_all | solution.py:56
  29.8 1.6 %copy-start.2 = (f32[1,1024]{1,0:T(1,128)S(1)}, f32[1,1024]{1,0:T(1,128)}, u32[]{:S(2)}) copy-start(f32[1,1024]{1,0:T(1,128)} %param.11) | copy-start | bytes 12292
  29.8 1.6 %copy-start.4 = (bf16[64,1,1024]{2,0,1:T(8,128)(2,1)S(1)}, bf16[64,1,1024]{2,0,1:T(8,128)(2,1)}, u32[]{:S(2)}) copy-start(bf16[64,1,1024]{2,0,1:T(8,128)(2,1)} %param.9) | copy-start | bytes 393220
  29.8 1.6 %copy-start.6 = (f32[1,1024]{1,0:T(1,128)S(1)}, f32[1,1024]{1,0:T(1,128)}, u32[]{:S(2)}) copy-start(f32[1,1024]{1,0:T(1,128)} %param.10) | copy-start | bytes 12292
  32.7 24.8 %all-to-all-start.1 = ((bf16[8,8,4096]{2,1,0:T(8,128)(2,1)}), bf16[8,8,4096]{2,1,0:T(8,128)(2,1)S(1)}, u32[]{:S(2)}, u32[]{:S(2)}) async-start(bf16[8,8,4096]{2,1,0:T(8,128)(2,1)} %broadcast_in_dim.43), calls=%async_computation.1 | async-start | bytes 1048576 | tf_op jit(solution)/shard_map/all_to_all | solution.py:74
  59.3 17.9 %copy-start = (f32[1,131072]{1,0:T(1,128)S(1)}, f32[1,131072]{1,0:T(1,128)}, u32[]{:S(2)}) copy-start(f32[1,131072]{1,0:T(1,128)} %param.8) | copy-start | bytes 1572868

commit v9 on v8

--- a/solution.py
+++ b/solution.py
@@ -79,7 +79,7 @@
     factor = taper_factors[0] / (members - 1)
     choose = block_links[..., None] == jnp.arange(obs_blocks, dtype=jnp.int32)
     localize = jnp.sum(jnp.where(choose, factor[..., None], jnp.float32(0.0)), axis=1)
-    localize_high = localize.astype(jnp.bfloat16)
+    localize_high = lax.optimization_barrier(localize.astype(jnp.bfloat16))
     localize_low = (localize - localize_high.astype(jnp.float32)).astype(jnp.bfloat16)
     ensemble = jnp.dot(localize_high, all_products, preferred_element_type=jnp.float32) + jnp.dot(
         localize_low, all_products, preferred_element_type=jnp.float32

time: 78.8 us -> 78.8 us (level)
  no operation moved by 1% of the time
where the time goes in v9:
time: 78.8 us; the launch traced here: 78.5 us
  waiting for transfers between devices  29.2 us (37%)
  starting transfers between devices  21.6 us (27%)
  blocking collectives  17.6 us (22%)
  other arithmetic  3.97 us (5%)
  matrix products  3.04 us (4%)
  local copies, waits for them, and re-layouts  2.23 us (3%)
  between operations  0.87 us (1%)
    all_to_all x1, blocking collectives, local(): lax.all_to_all(increment_low, 'slab', split_axis=0, concat_axis=0, tiled=...  17.6 us
    all_to_all x1, waiting for transfers between devices, local(): lax.all_to_all(copies, 'obs', split_axis=0, concat_axis=0, tiled=True)  16.9 us
    all_to_all x1, starting transfers between devices, local(): lax.all_to_all(pieces, 'slab', split_axis=0, concat_axis=0, tiled=True)  14.8 us
    all_to_all x1, waiting for transfers between devices, local(): lax.all_to_all(pieces, 'slab', split_axis=0, concat_axis=0, tiled=True)  12.2 us
    all_to_all x1, starting transfers between devices, local(): lax.all_to_all(copies, 'obs', split_axis=0, concat_axis=0, tiled=True)  6.82 us
    unnamed x1, other arithmetic  1.82 us
  transfers between devices with their start and end apart: 2, of which 2 were waited for; matrix products, arithmetic and copies ran while one was open for 1% of the time, Pallas kernels for 0%

profile of v9, /device:TPU:1, one launch (start us, length us, event | category | flops | bytes accessed | tf_op | source)
XLA Modules:
  0.0 78.5 jit_solution(17737815865834571496)
XLA Ops:
  0.0 0.0 copy-start.3
  0.0 0.0 copy-start.1
  0.0 0.0 copy-start.5
  0.0 1.8 %convert.14 = bf16[64,16,128]{2,1,0:T(8,128)(2,1)} convert(f32[64,16,128]{2,1,0:T(8,128)} %bitcast.63) | non-fusion elementwise | flops 131072 | bytes 786432
  1.8 14.8 %all-to-all-start = ((bf16[64,16,128]{2,1,0:T(8,128)(2,1)}), bf16[64,16,128]{2,1,0:T(8,128)(2,1)S(1)}, u32[]{:S(2)}, u32[]{:S(2)}) async-start(bf16[64,16,128]{2,1,0:T(8,128)(2,1)} %convert.14), calls=%async_computation | async-start | bytes 524288 | tf_op jit(solution)/shard_map/all_to_all | solution.py:56
  17.3 0.0 copy-done.3
  17.3 0.1 copy.23
  17.4 0.0 copy-done.1
  17.4 0.1 copy.22
  17.5 12.2 %all-to-all-done = bf16[64,16,128]{2,1,0:T(8,128)(2,1)S(1)} async-done(((bf16[64,16,128]{2,1,0:T(8,128)(2,1)}), bf16[64,16,128]{2,1,0:T(8,128)(2,1)S(1)}, u32[]{:S(2)}, u32[]{:S(2)}) %all-to-all-start) | async-done | bytes 262176 | tf_op jit(solution)/shard_map/all_to_all | solution.py:56
  29.7 0.1 copy.39
  29.8 0.0 copy-done.5
  29.8 0.0 copy-start.2
  29.8 0.0 copy-start.4
  29.8 0.0 copy-start.6
  29.9 1.5 %fusion.16 = (f32[1024]{0:T(1024)S(1)}, f32[1024,64]{0,1:T(8,128)S(1)}) fusion(bf16[64,2048]{1,0:T(8,128)(2,1)S(1)} %bitcast.66, s32[1024]{0:T(1024)S(1)} %bitcast.72), kind=kOutput, calls=%fused_computation.34 | convolution fusion | flops 270597120 | bytes 532480 | tf_op jit(solution)/shard_map/dot_general | solution.py:26
  31.3 0.1 multiply_reduce_fusion
  31.4 0.0 copy-done.2
  31.4 0.0 copy-done.4
  31.4 0.0 copy-done.6
  31.4 0.2 convolution_convert_fusion.1
  31.7 0.2 broadcast_in_dim.42
  31.8 0.8 %broadcast_in_dim.43 = bf16[8,8,4096]{2,1,0:T(8,128)(2,1)} broadcast(bf16[8,4096]{1,0:T(8,128)(2,1)S(1)} %broadcast_in_dim.42), dimensions={1,2} | broadcast | bytes 589824 | tf_op jit(solution)/shard_map/broadcast_in_dim | solution.py:73
  32.7 6.8 %all-to-all-start.1 = ((bf16[8,8,4096]{2,1,0:T(8,128)(2,1)}), bf16[8,8,4096]{2,1,0:T(8,128)(2,1)S(1)}, u32[]{:S(2)}, u32[]{:S(2)}) async-start(bf16[8,8,4096]{2,1,0:T(8,128)(2,1)} %broadcast_in_dim.43), calls=%async_computation.1 | async-start | bytes 1048576 | tf_op jit(solution)/shard_map/all_to_all | solution.py:74
  39.5 0.1 select_reduce_fusion
  39.7 0.3 copy.21
  39.9 0.2 convert_reduce_fusion
  40.2 0.3 convert_subtract_fusion
  40.5 16.9 %all-to-all-done.1 = bf16[8,8,4096]{2,1,0:T(8,128)(2,1)S(1)} async-done(((bf16[8,8,4096]{2,1,0:T(8,128)(2,1)}), bf16[8,8,4096]{2,1,0:T(8,128)(2,1)S(1)}, u32[]{:S(2)}, u32[]{:S(2)}) %all-to-all-start.1) | async-done | bytes 524320 | tf_op jit(solution)/shard_map/all_to_all | solution.py:74
  57.4 0.2 fusion.3
  57.7 0.2 convolution_add_fusion
  57.9 0.4 reshape.76
  58.3 1.0 %convolution_convert_fusion = bf16[32,64,64]{2,1,0:T(8,128)(2,1)S(1)} fusion(f32[64,32,64]{0,2,1:T(8,128)S(1)} %bitcast.62, f32[32,64,64]{2,1,0:T(8,128)S(1)} %reshape.76), kind=kOutput, calls=%fused_computation.6 | convolution fusion | flops 50462720 | bytes 1310720 | tf_op jit(solution)/shard_map/bmn,nbp->mbp/dot_general | solution.py:89
  59.3 0.0 copy-start
  59.3 0.3 copy.26
  59.6 17.6 %all_to_all.15 = bf16[64,16,128]{2,1,0:T(8,128)(2,1)S(1)} all-to-all(bf16[64,16,128]{2,1,0:T(8,128)(2,1)S(1)} %copy.26), channel_id=1, replica_groups=mesh['slab'=64,'obs'=8] {'slab'}, dimensions={0} | all-to-all | bytes 524288 | tf_op jit(solution)/shard_map/all_to_all | solution.py:91
  77.2 0.0 copy-done
  77.2 1.3 %add.24 = f32[1,131072]{1,0:T(1,128)} add(f32[1,131072]{1,0:T(1,128)S(1)} %copy-done, f32[1,131072]{1,0:T(1,128)S(1)} %bitcast.65) | non-fusion elementwise | flops 131072 | bytes 1572864 | tf_op jit(solution)/shard_map/add | solution.py:92
  (8 shorter events, 0.1 us)
Async XLA Ops:
  0.0 17.3 %copy-start.3 = (f32[1,32,8]{1,2,0:T(8,128)S(1)}, f32[1,32,8]{1,2,0:T(8,128)}, u32[]{:S(2)}) copy-start(f32[1,32,8]{1,2,0:T(8,128)} %param.15) | copy-start | bytes 3076
  0.0 17.4 %copy-start.1 = (s32[1,32,8]{1,2,0:T(8,128)S(1)}, s32[1,32,8]{1,2,0:T(8,128)}, u32[]{:S(2)}) copy-start(s32[1,32,8]{1,2,0:T(8,128)} %param.14) | copy-start | bytes 3076
  0.0 29.8 %copy-start.5 = (s32[1,1024]{1,0:T(1,128)S(1)}, s32[1,1024]{1,0:T(1,128)}, u32[]{:S(2)}) copy-start(s32[1,1024]{1,0:T(1,128)} %param.12) | copy-start | bytes 12292
  1.8 27.9 %all-to-all-start = ((bf16[64,16,128]{2,1,0:T(8,128)(2,1)}), bf16[64,16,128]{2,1,0:T(8,128)(2,1)S(1)}, u32[]{:S(2)}, u32[]{:S(2)}) async-start(bf16[64,16,128]{2,1,0:T(8,128)(2,1)} %convert.14), calls=%async_computation | async-start | bytes 524288 | tf_op jit(solution)/shard_map/all_to_all | solution.py:56
  29.8 1.6 %copy-start.2 = (f32[1,1024]{1,0:T(1,128)S(1)}, f32[1,1024]{1,0:T(1,128)}, u32[]{:S(2)}) copy-start(f32[1,1024]{1,0:T(1,128)} %param.11) | copy-start | bytes 12292
  29.8 1.6 %copy-start.4 = (bf16[64,1,1024]{2,0,1:T(8,128)(2,1)S(1)}, bf16[64,1,1024]{2,0,1:T(8,128)(2,1)}, u32[]{:S(2)}) copy-start(bf16[64,1,1024]{2,0,1:T(8,128)(2,1)} %param.9) | copy-start | bytes 393220
  29.8 1.6 %copy-start.6 = (f32[1,1024]{1,0:T(1,128)S(1)}, f32[1,1024]{1,0:T(1,128)}, u32[]{:S(2)}) copy-start(f32[1,1024]{1,0:T(1,128)} %param.10) | copy-start | bytes 12292
  32.7 24.8 %all-to-all-start.1 = ((bf16[8,8,4096]{2,1,0:T(8,128)(2,1)}), bf16[8,8,4096]{2,1,0:T(8,128)(2,1)S(1)}, u32[]{:S(2)}, u32[]{:S(2)}) async-start(bf16[8,8,4096]{2,1,0:T(8,128)(2,1)} %broadcast_in_dim.43), calls=%async_computation.1 | async-start | bytes 1048576 | tf_op jit(solution)/shard_map/all_to_all | solution.py:74
  59.3 17.9 %copy-start = (f32[1,131072]{1,0:T(1,128)S(1)}, f32[1,131072]{1,0:T(1,128)}, u32[]{:S(2)}) copy-start(f32[1,131072]{1,0:T(1,128)} %param.8) | copy-start | bytes 1572868

commit v10 on v9

--- a/solution.py
+++ b/solution.py
@@ -54,8 +54,9 @@
     lanes = 128
     pieces = background_members.reshape(members, -1, lanes)
     tile = lax.all_to_all(pieces, "slab", split_axis=0, concat_axis=0, tiled=True)
-    tile_low = lax.optimization_barrier(tile.reshape(members, -1).astype(jnp.bfloat16))
-    tile_work = tile_low.astype(jnp.float32)
+    tile_work = lax.reduce_precision(tile.reshape(members, -1), exponent_bits=8, mantissa_bits=7)
+    tile_work = lax.optimization_barrier(tile_work)
+    tile_low = tile_work.astype(jnp.bfloat16)
     blocks = coupling_listing.shape[1]
     deviation = tile_work - jnp.mean(tile_work, axis=0, keepdims=True)
 

time: 78.8 us -> 82.6 us (1.048)
  waiting for transfers between devices: 29.2 us -> 33.9 us
  other arithmetic: 3.97 us -> 2.01 us
    all_to_all x1, waiting for transfers between devices: 12.2 us -> 17 us  [local(): lax.all_to_all(pieces, 'slab', split_axis=0, concat_axis=0, tiled=True)]
    unnamed x1 -> x0, other arithmetic: 1.82 us -> none
where the time goes in v10:
time: 82.6 us; the launch traced here: 82.3 us
  waiting for transfers between devices  33.9 us (41%)
  starting transfers between devices  21.6 us (26%)
  blocking collectives  18.3 us (22%)
  matrix products  3.16 us (4%)
  local copies, waits for them, and re-layouts  2.38 us (3%)
  other arithmetic  2.01 us (2%)
  between operations  0.91 us (1%)
    all_to_all x1, blocking collectives, local(): lax.all_to_all(increment_low, 'slab', split_axis=0, concat_axis=0, tiled=...  18.3 us
    all_to_all x1, waiting for transfers between devices, local(): lax.all_to_all(pieces, 'slab', split_axis=0, concat_axis=0, tiled=True)  17 us
    all_to_all x1, waiting for transfers between devices, local(): lax.all_to_all(copies, 'obs', split_axis=0, concat_axis=0, tiled=True)  16.9 us
    all_to_all x1, starting transfers between devices, local(): lax.all_to_all(pieces, 'slab', split_axis=0, concat_axis=0, tiled=True)  14.8 us
    all_to_all x1, starting transfers between devices, local(): lax.all_to_all(copies, 'obs', split_axis=0, concat_axis=0, tiled=True)  6.82 us
  transfers between devices with their start and end apart: 2, of which 2 were waited for; matrix products, arithmetic and copies ran while one was open for 1% of the time, Pallas kernels for 0%

profile of v10, /device:TPU:1, one launch (start us, length us, event | category | flops | bytes accessed | tf_op | source)
XLA Modules:
  0.0 82.3 jit_solution(3387866770332306600)
XLA Ops:
  0.0 14.8 %all-to-all-start = ((f32[64,16,128]{2,1,0:T(8,128)}), f32[64,16,128]{2,1,0:T(8,128)S(1)}, u32[]{:S(2)}, u32[]{:S(2)}) async-start(f32[64,16,128]{2,1,0:T(8,128)} %bitcast.65), calls=%async_computation | async-start | bytes 1048576 | tf_op jit(solution)/shard_map/all_to_all | solution.py:56
  15.5 0.0 copy-start.5
  15.5 17.0 %all-to-all-done = f32[64,16,128]{2,1,0:T(8,128)S(1)} async-done(((f32[64,16,128]{2,1,0:T(8,128)}), f32[64,16,128]{2,1,0:T(8,128)S(1)}, u32[]{:S(2)}, u32[]{:S(2)}) %all-to-all-start) | async-done | bytes 524320 | tf_op jit(solution)/shard_map/all_to_all | solution.py:56
  32.6 0.2 copy.39
  32.7 0.0 copy-done.5
  32.7 0.0 copy-start.1
  32.8 0.0 copy-start.4
  32.8 0.0 copy-start.6
  32.8 1.6 %fusion.17 = (f32[1024]{0:T(1024)S(1)}, f32[1024,64]{0,1:T(8,128)S(1)}) fusion(f32[64,2048]{1,0:T(8,128)S(1)} %bitcast.61, s32[1024]{0:T(1024)S(1)} %bitcast.72), kind=kOutput, calls=%fused_computation.34 | convolution fusion | flops 270728192 | bytes 794624 | tf_op jit(solution)/shard_map/dot_general | solution.py:26
  34.4 0.1 multiply_reduce_fusion
  34.4 0.0 copy-done.1
  34.5 0.0 copy-done.4
  34.5 0.0 copy-done.6
  34.5 0.2 convolution_convert_fusion.1
  34.7 0.0 copy-start.3
  34.7 0.0 copy-start.2
  34.7 0.2 broadcast_in_dim.42
  34.9 0.8 %broadcast_in_dim.43 = bf16[8,8,4096]{2,1,0:T(8,128)(2,1)} broadcast(bf16[8,4096]{1,0:T(8,128)(2,1)S(1)} %broadcast_in_dim.42), dimensions={1,2} | broadcast | bytes 589824 | tf_op jit(solution)/shard_map/broadcast_in_dim | solution.py:74
  35.7 6.8 %all-to-all-start.1 = ((bf16[8,8,4096]{2,1,0:T(8,128)(2,1)}), bf16[8,8,4096]{2,1,0:T(8,128)(2,1)S(1)}, u32[]{:S(2)}, u32[]{:S(2)}) async-start(bf16[8,8,4096]{2,1,0:T(8,128)(2,1)} %broadcast_in_dim.43), calls=%async_computation.1 | async-start | bytes 1048576 | tf_op jit(solution)/shard_map/all_to_all | solution.py:75
  42.6 0.0 copy-done.3
  42.6 0.1 copy.23
  42.6 0.0 copy-done.2
  42.6 0.1 copy.22
  42.7 0.1 select_reduce_fusion
  42.9 0.3 copy.21
  43.3 0.3 broadcast_subtract_fusion
  43.6 16.9 %all-to-all-done.1 = bf16[8,8,4096]{2,1,0:T(8,128)(2,1)S(1)} async-done(((bf16[8,8,4096]{2,1,0:T(8,128)(2,1)}), bf16[8,8,4096]{2,1,0:T(8,128)(2,1)S(1)}, u32[]{:S(2)}, u32[]{:S(2)}) %all-to-all-start.1) | async-done | bytes 524320 | tf_op jit(solution)/shard_map/all_to_all | solution.py:75
  60.5 0.2 fusion.3
  60.7 0.2 convolution_add_fusion
  60.9 0.4 reshape.76
  61.4 1.0 %convolution_convert_fusion = bf16[32,64,64]{2,1,0:T(8,128)(2,1)S(1)} fusion(f32[64,32,64]{0,2,1:T(8,128)S(1)} %bitcast.64, f32[32,64,64]{2,1,0:T(8,128)S(1)} %reshape.76), kind=kOutput, calls=%fused_computation.4 | convolution fusion | flops 50462720 | bytes 1310720 | tf_op jit(solution)/shard_map/bmn,nbp->mbp/dot_general | solution.py:90
  62.3 0.0 copy-start
  62.3 0.3 copy.26
  62.6 18.3 %all_to_all.15 = bf16[64,16,128]{2,1,0:T(8,128)(2,1)S(1)} all-to-all(bf16[64,16,128]{2,1,0:T(8,128)(2,1)S(1)} %copy.26), channel_id=1, replica_groups=mesh['slab'=64,'obs'=8] {'slab'}, dimensions={0} | all-to-all | bytes 524288 | tf_op jit(solution)/shard_map/all_to_all | solution.py:92
  81.0 0.0 copy-done
  81.0 1.3 %add.24 = f32[1,131072]{1,0:T(1,128)} add(f32[1,131072]{1,0:T(1,128)S(1)} %copy-done, f32[1,131072]{1,0:T(1,128)S(1)} %bitcast.67) | non-fusion elementwise | flops 131072 | bytes 1572864 | tf_op jit(solution)/shard_map/add | solution.py:93
  (10 shorter events, 0.1 us)
Async XLA Ops:
  0.0 32.5 %all-to-all-start = ((f32[64,16,128]{2,1,0:T(8,128)}), f32[64,16,128]{2,1,0:T(8,128)S(1)}, u32[]{:S(2)}, u32[]{:S(2)}) async-start(f32[64,16,128]{2,1,0:T(8,128)} %bitcast.65), calls=%async_computation | async-start | bytes 1048576 | tf_op jit(solution)/shard_map/all_to_all | solution.py:56
  15.5 17.2 %copy-start.5 = (s32[1,1024]{1,0:T(1,128)S(1)}, s32[1,1024]{1,0:T(1,128)}, u32[]{:S(2)}) copy-start(s32[1,1024]{1,0:T(1,128)} %param.12) | copy-start | bytes 12292
  32.7 1.7 %copy-start.1 = (f32[1,1024]{1,0:T(1,128)S(1)}, f32[1,1024]{1,0:T(1,128)}, u32[]{:S(2)}) copy-start(f32[1,1024]{1,0:T(1,128)} %param.11) | copy-start | bytes 12292
  32.8 1.7 %copy-start.4 = (bf16[64,1,1024]{2,0,1:T(8,128)(2,1)S(1)}, bf16[64,1,1024]{2,0,1:T(8,128)(2,1)}, u32[]{:S(2)}) copy-start(bf16[64,1,1024]{2,0,1:T(8,128)(2,1)} %param.9) | copy-start | bytes 393220
  32.8 1.7 %copy-start.6 = (f32[1,1024]{1,0:T(1,128)S(1)}, f32[1,1024]{1,0:T(1,128)}, u32[]{:S(2)}) copy-start(f32[1,1024]{1,0:T(1,128)} %param.10) | copy-start | bytes 12292
  34.7 7.9 %copy-start.3 = (f32[1,32,8]{1,2,0:T(8,128)S(1)}, f32[1,32,8]{1,2,0:T(8,128)}, u32[]{:S(2)}) copy-start(f32[1,32,8]{1,2,0:T(8,128)} %param.15) | copy-start | bytes 3076
  34.7 7.9 %copy-start.2 = (s32[1,32,8]{1,2,0:T(8,128)S(1)}, s32[1,32,8]{1,2,0:T(8,128)}, u32[]{:S(2)}) copy-start(s32[1,32,8]{1,2,0:T(8,128)} %param.14) | copy-start | bytes 3076
  35.7 24.8 %all-to-all-start.1 = ((bf16[8,8,4096]{2,1,0:T(8,128)(2,1)}), bf16[8,8,4096]{2,1,0:T(8,128)(2,1)S(1)}, u32[]{:S(2)}, u32[]{:S(2)}) async-start(bf16[8,8,4096]{2,1,0:T(8,128)(2,1)} %broadcast_in_dim.43), calls=%async_computation.1 | async-start | bytes 1048576 | tf_op jit(solution)/shard_map/all_to_all | solution.py:75
  62.3 18.6 %copy-start = (f32[1,131072]{1,0:T(1,128)S(1)}, f32[1,131072]{1,0:T(1,128)}, u32[]{:S(2)}) copy-start(f32[1,131072]{1,0:T(1,128)} %param.8) | copy-start | bytes 1572868

commit v11 on v9

--- a/solution.py
+++ b/solution.py
@@ -89,7 +89,8 @@
     increment = jnp.einsum("bmn,nbp->mbp", ensemble, region_dev, precision=lax.Precision.HIGH)
     increment_low = increment.reshape(members, -1, lanes).astype(jnp.bfloat16)
     back = lax.all_to_all(increment_low, "slab", split_axis=0, concat_axis=0, tiled=True)
-    return background_members + back.reshape(background_members.shape).astype(jnp.float32)
+    analysis = pieces + back.astype(jnp.float32)
+    return analysis.reshape(background_members.shape)
 
 
 def solution(mesh):

time: 78.8 us -> 78.3 us (level)
  other arithmetic: 3.97 us -> 3 us
where the time goes in v11:
time: 78.3 us; the launch traced here: 78 us
  waiting for transfers between devices  29.6 us (38%)
  starting transfers between devices  21.6 us (28%)
  blocking collectives  17.6 us (22%)
  matrix products  3.06 us (4%)
  other arithmetic  3 us (4%)
  local copies, waits for them, and re-layouts  2.29 us (3%)
  between operations  0.87 us (1%)
    all_to_all x1, blocking collectives, local(): lax.all_to_all(increment_low, 'slab', split_axis=0, concat_axis=0, tiled=...  17.6 us
    all_to_all x1, waiting for transfers between devices, local(): lax.all_to_all(copies, 'obs', split_axis=0, concat_axis=0, tiled=True)  17.3 us
    all_to_all x1, starting transfers between devices, local(): lax.all_to_all(pieces, 'slab', split_axis=0, concat_axis=0, tiled=True)  14.8 us
    all_to_all x1, waiting for transfers between devices, local(): lax.all_to_all(pieces, 'slab', split_axis=0, concat_axis=0, tiled=True)  12.2 us
    all_to_all x1, starting transfers between devices, local(): lax.all_to_all(copies, 'obs', split_axis=0, concat_axis=0, tiled=True)  6.82 us
    unnamed x1, other arithmetic  1.82 us
  transfers between devices with their start and end apart: 2, of which 2 were waited for; matrix products, arithmetic and copies ran while one was open for 1% of the time, Pallas kernels for 0%

profile of v11, /device:TPU:1, one launch (start us, length us, event | category | flops | bytes accessed | tf_op | source)
XLA Modules:
  0.0 78.0 jit_solution(8903954572104922643)
XLA Ops:
  0.0 0.0 copy-start.3
  0.0 0.0 copy-start.1
  0.0 0.0 copy-start.5
  0.0 1.8 %convert.13 = bf16[64,16,128]{2,1,0:T(8,128)(2,1)} convert(f32[64,16,128]{2,1,0:T(8,128)} %bitcast.67) | non-fusion elementwise | flops 131072 | bytes 786432
  1.8 14.8 %all-to-all-start = ((bf16[64,16,128]{2,1,0:T(8,128)(2,1)}), bf16[64,16,128]{2,1,0:T(8,128)(2,1)S(1)}, u32[]{:S(2)}, u32[]{:S(2)}) async-start(bf16[64,16,128]{2,1,0:T(8,128)(2,1)} %convert.13), calls=%async_computation | async-start | bytes 524288 | tf_op jit(solution)/shard_map/all_to_all | solution.py:56
  17.3 0.0 copy-done.3
  17.3 0.1 copy.24
  17.4 0.0 copy-done.1
  17.4 0.1 copy.23
  17.5 12.2 %all-to-all-done = bf16[64,16,128]{2,1,0:T(8,128)(2,1)S(1)} async-done(((bf16[64,16,128]{2,1,0:T(8,128)(2,1)}), bf16[64,16,128]{2,1,0:T(8,128)(2,1)S(1)}, u32[]{:S(2)}, u32[]{:S(2)}) %all-to-all-start) | async-done | bytes 262176 | tf_op jit(solution)/shard_map/all_to_all | solution.py:56
  29.7 0.1 copy.40
  29.8 0.0 copy-done.5
  29.8 0.0 copy-start.2
  29.8 0.0 copy-start.4
  29.8 0.0 copy-start.6
  29.9 1.5 %fusion.16 = (f32[1024]{0:T(1024)S(1)}, f32[1024,64]{0,1:T(8,128)S(1)}) fusion(bf16[64,2048]{1,0:T(8,128)(2,1)S(1)} %bitcast.63, s32[1024]{0:T(1024)S(1)} %bitcast.73), kind=kOutput, calls=%fused_computation.35 | convolution fusion | flops 270597120 | bytes 532480 | tf_op jit(solution)/shard_map/dot_general | solution.py:26
  31.3 0.1 multiply_reduce_fusion
  31.4 0.0 copy-done.2
  31.4 0.0 copy-done.4
  31.4 0.0 copy-done.6
  31.4 0.2 convolution_convert_fusion.1
  31.7 0.2 broadcast_in_dim.42
  31.9 0.8 %broadcast_in_dim.43 = bf16[8,8,4096]{2,1,0:T(8,128)(2,1)} broadcast(bf16[8,4096]{1,0:T(8,128)(2,1)S(1)} %broadcast_in_dim.42), dimensions={1,2} | broadcast | bytes 589824 | tf_op jit(solution)/shard_map/broadcast_in_dim | solution.py:73
  32.7 6.8 %all-to-all-start.1 = ((bf16[8,8,4096]{2,1,0:T(8,128)(2,1)}), bf16[8,8,4096]{2,1,0:T(8,128)(2,1)S(1)}, u32[]{:S(2)}, u32[]{:S(2)}) async-start(bf16[8,8,4096]{2,1,0:T(8,128)(2,1)} %broadcast_in_dim.43), calls=%async_computation.1 | async-start | bytes 1048576 | tf_op jit(solution)/shard_map/all_to_all | solution.py:74
  39.5 0.1 select_reduce_fusion
  39.7 0.1 convert_reduce_fusion
  39.8 0.3 copy.22
  40.1 17.3 %all-to-all-done.1 = bf16[8,8,4096]{2,1,0:T(8,128)(2,1)S(1)} async-done(((bf16[8,8,4096]{2,1,0:T(8,128)(2,1)}), bf16[8,8,4096]{2,1,0:T(8,128)(2,1)S(1)}, u32[]{:S(2)}, u32[]{:S(2)}) %all-to-all-start.1) | async-done | bytes 524320 | tf_op jit(solution)/shard_map/all_to_all | solution.py:74
  57.5 0.2 fusion.3
  57.7 0.2 convolution_add_fusion
  57.9 0.4 reshape.64
  58.3 1.0 %convolution_convert_fusion = bf16[32,64,64]{2,1,0:T(8,128)(2,1)S(1)} fusion(f32[64,32,64]{0,2,1:T(8,128)S(1)} %bitcast.62, f32[32,64,64]{2,1,0:T(8,128)S(1)} %reshape.64), kind=kOutput, calls=%fused_computation.4 | convolution fusion | flops 50462720 | bytes 1310720 | tf_op jit(solution)/shard_map/bmn,nbp->mbp/dot_general | solution.py:89
  59.3 0.0 copy-start
  59.3 0.3 copy.27
  59.6 17.6 %all_to_all.15 = bf16[64,16,128]{2,1,0:T(8,128)(2,1)S(1)} all-to-all(bf16[64,16,128]{2,1,0:T(8,128)(2,1)S(1)} %copy.27), channel_id=1, replica_groups=mesh['slab'=64,'obs'=8] {'slab'}, dimensions={0} | all-to-all | bytes 524288 | tf_op jit(solution)/shard_map/all_to_all | solution.py:91
  77.2 0.0 copy-done
  77.2 0.9 %convert_add_fusion = f32[64,16,128]{2,1,0:T(8,128)} fusion(f32[64,16,128]{2,1,0:T(8,128)S(1)} %bitcast.68, bf16[64,16,128]{2,1,0:T(8,128)(2,1)S(1)} %all_to_all.15), kind=kLoop, calls=%fused_computation.11 | loop fusion | flops 262144 | bytes 1310720 | tf_op jit(solution)/shard_map/add | solution.py:92
  (8 shorter events, 0.1 us)
Async XLA Ops:
  0.0 17.3 %copy-start.3 = (f32[1,32,8]{1,2,0:T(8,128)S(1)}, f32[1,32,8]{1,2,0:T(8,128)}, u32[]{:S(2)}) copy-start(f32[1,32,8]{1,2,0:T(8,128)} %param.15) | copy-start | bytes 3076
  0.0 17.4 %copy-start.1 = (s32[1,32,8]{1,2,0:T(8,128)S(1)}, s32[1,32,8]{1,2,0:T(8,128)}, u32[]{:S(2)}) copy-start(s32[1,32,8]{1,2,0:T(8,128)} %param.14) | copy-start | bytes 3076
  0.0 29.8 %copy-start.5 = (s32[1,1024]{1,0:T(1,128)S(1)}, s32[1,1024]{1,0:T(1,128)}, u32[]{:S(2)}) copy-start(s32[1,1024]{1,0:T(1,128)} %param.12) | copy-start | bytes 12292
  1.8 27.9 %all-to-all-start = ((bf16[64,16,128]{2,1,0:T(8,128)(2,1)}), bf16[64,16,128]{2,1,0:T(8,128)(2,1)S(1)}, u32[]{:S(2)}, u32[]{:S(2)}) async-start(bf16[64,16,128]{2,1,0:T(8,128)(2,1)} %convert.13), calls=%async_computation | async-start | bytes 524288 | tf_op jit(solution)/shard_map/all_to_all | solution.py:56
  29.8 1.6 %copy-start.2 = (f32[1,1024]{1,0:T(1,128)S(1)}, f32[1,1024]{1,0:T(1,128)}, u32[]{:S(2)}) copy-start(f32[1,1024]{1,0:T(1,128)} %param.11) | copy-start | bytes 12292
  29.8 1.6 %copy-start.4 = (bf16[64,1,1024]{2,0,1:T(8,128)(2,1)S(1)}, bf16[64,1,1024]{2,0,1:T(8,128)(2,1)}, u32[]{:S(2)}) copy-start(bf16[64,1,1024]{2,0,1:T(8,128)(2,1)} %param.9) | copy-start | bytes 393220
  29.8 1.6 %copy-start.6 = (f32[1,1024]{1,0:T(1,128)S(1)}, f32[1,1024]{1,0:T(1,128)}, u32[]{:S(2)}) copy-start(f32[1,1024]{1,0:T(1,128)} %param.10) | copy-start | bytes 12292
  32.7 24.8 %all-to-all-start.1 = ((bf16[8,8,4096]{2,1,0:T(8,128)(2,1)}), bf16[8,8,4096]{2,1,0:T(8,128)(2,1)S(1)}, u32[]{:S(2)}, u32[]{:S(2)}) async-start(bf16[8,8,4096]{2,1,0:T(8,128)(2,1)} %broadcast_in_dim.43), calls=%async_computation.1 | async-start | bytes 1048576 | tf_op jit(solution)/shard_map/all_to_all | solution.py:74
  59.3 17.9 %copy-start = (f32[1,131072]{1,0:T(1,128)S(1)}, f32[1,131072]{1,0:T(1,128)}, u32[]{:S(2)}) copy-start(f32[1,131072]{1,0:T(1,128)} %param.8) | copy-start | bytes 1572868

commit v12 on v11

--- a/solution.py
+++ b/solution.py
@@ -69,10 +69,11 @@
         active_tallies,
     )
     groups = lax.axis_size("obs")
-    flat = products.astype(jnp.bfloat16).reshape(products.shape[0], -1)
+    block_size = products.shape[1] * products.shape[2]
+    flat = products.astype(jnp.bfloat16).reshape(16, -1)
     copies = jnp.broadcast_to(flat[None], (groups,) + flat.shape)
     all_products = lax.all_to_all(copies, "obs", split_axis=0, concat_axis=0, tiled=True)
-    all_products = all_products.reshape(-1, flat.shape[1])
+    all_products = all_products.reshape(-1, block_size)
     obs_blocks = all_products.shape[0]
 
     block_links = coupling_listing[0]

time: 78.3 us -> 78.5 us (level)
  no operation moved by 1% of the time
where the time goes in v12:
time: 78.5 us; the launch traced here: 78.2 us
  waiting for transfers between devices  29.6 us (38%)
  starting transfers between devices  21.6 us (28%)
  blocking collectives  17.6 us (22%)
  matrix products  3.05 us (4%)
  other arithmetic  3 us (4%)
  local copies, waits for them, and re-layouts  2.47 us (3%)
  between operations  0.88 us (1%)
    all_to_all x1, blocking collectives, local(): lax.all_to_all(increment_low, 'slab', split_axis=0, concat_axis=0, tiled=...  17.6 us
    all_to_all x1, waiting for transfers between devices, local(): lax.all_to_all(copies, 'obs', split_axis=0, concat_axis=0, tiled=True)  17.3 us
    all_to_all x1, starting transfers between devices, local(): lax.all_to_all(pieces, 'slab', split_axis=0, concat_axis=0, tiled=True)  14.8 us
    all_to_all x1, waiting for transfers between devices, local(): lax.all_to_all(pieces, 'slab', split_axis=0, concat_axis=0, tiled=True)  12.2 us
    all_to_all x1, starting transfers between devices, local(): lax.all_to_all(copies, 'obs', split_axis=0, concat_axis=0, tiled=True)  6.82 us
    unnamed x1, other arithmetic  1.82 us
  transfers between devices with their start and end apart: 2, of which 2 were waited for; matrix products, arithmetic and copies ran while one was open for 1% of the time, Pallas kernels for 0%

profile of v12, /device:TPU:1, one launch (start us, length us, event | category | flops | bytes accessed | tf_op | source)
XLA Modules:
  0.0 78.2 jit_solution(7629128041511100261)
XLA Ops:
  0.0 0.0 copy-start.3
  0.0 0.0 copy-start.1
  0.0 0.0 copy-start.5
  0.0 1.8 %convert.13 = bf16[64,16,128]{2,1,0:T(8,128)(2,1)} convert(f32[64,16,128]{2,1,0:T(8,128)} %bitcast.64) | non-fusion elementwise | flops 131072 | bytes 786432
  1.8 14.8 %all-to-all-start = ((bf16[64,16,128]{2,1,0:T(8,128)(2,1)}), bf16[64,16,128]{2,1,0:T(8,128)(2,1)S(1)}, u32[]{:S(2)}, u32[]{:S(2)}) async-start(bf16[64,16,128]{2,1,0:T(8,128)(2,1)} %convert.13), calls=%async_computation | async-start | bytes 524288 | tf_op jit(solution)/shard_map/all_to_all | solution.py:56
  17.3 0.0 copy-done.3
  17.3 0.1 copy.24
  17.4 0.0 copy-done.1
  17.4 0.1 copy.23
  17.5 12.2 %all-to-all-done = bf16[64,16,128]{2,1,0:T(8,128)(2,1)S(1)} async-done(((bf16[64,16,128]{2,1,0:T(8,128)(2,1)}), bf16[64,16,128]{2,1,0:T(8,128)(2,1)S(1)}, u32[]{:S(2)}, u32[]{:S(2)}) %all-to-all-start) | async-done | bytes 262176 | tf_op jit(solution)/shard_map/all_to_all | solution.py:56
  29.7 0.1 copy.40
  29.8 0.0 copy-done.5
  29.8 0.0 copy-start.2
  29.8 0.0 copy-start.4
  29.8 0.0 copy-start.6
  29.9 1.5 %fusion.13 = (f32[1024]{0:T(1024)S(1)}, f32[1024,64]{0,1:T(8,128)S(1)}) fusion(bf16[64,2048]{1,0:T(8,128)(2,1)S(1)} %bitcast.60, s32[1024]{0:T(1024)S(1)} %bitcast.70), kind=kOutput, calls=%fused_computation.32 | convolution fusion | flops 270597120 | bytes 532480 | tf_op jit(solution)/shard_map/dot_general | solution.py:26
  31.3 0.1 multiply_reduce_fusion
  31.4 0.0 copy-done.2
  31.4 0.0 copy-done.4
  31.4 0.0 copy-done.6
  31.4 0.2 convolution_convert_fusion.1
  31.7 0.2 broadcast_in_dim.42
  31.8 0.8 %broadcast_in_dim.43 = bf16[8,16,2048]{2,1,0:T(8,128)(2,1)} broadcast(bf16[16,2048]{1,0:T(8,128)(2,1)S(1)} %broadcast_in_dim.42), dimensions={1,2} | broadcast | bytes 589824 | tf_op jit(solution)/shard_map/broadcast_in_dim | solution.py:74
  32.7 6.8 %all-to-all-start.1 = ((bf16[8,16,2048]{2,1,0:T(8,128)(2,1)}), bf16[8,16,2048]{2,1,0:T(8,128)(2,1)S(1)}, u32[]{:S(2)}, u32[]{:S(2)}) async-start(bf16[8,16,2048]{2,1,0:T(8,128)(2,1)} %broadcast_in_dim.43), calls=%async_computation.1 | async-start | bytes 1048576 | tf_op jit(solution)/shard_map/all_to_all | solution.py:75
  39.5 0.1 select_reduce_fusion
  39.7 0.1 convert_reduce_fusion
  39.8 0.3 copy.22
  40.1 17.3 %all-to-all-done.1 = bf16[8,16,2048]{2,1,0:T(8,128)(2,1)S(1)} async-done(((bf16[8,16,2048]{2,1,0:T(8,128)(2,1)}), bf16[8,16,2048]{2,1,0:T(8,128)(2,1)S(1)}, u32[]{:S(2)}, u32[]{:S(2)}) %all-to-all-start.1) | async-done | bytes 524320 | tf_op jit(solution)/shard_map/all_to_all | solution.py:75
  57.5 0.2 reshape.63
  57.6 0.2 fusion.14
  57.9 0.2 convolution_add_fusion
  58.1 0.4 reshape.64
  58.5 1.0 %convolution_convert_fusion = bf16[32,64,64]{2,1,0:T(8,128)(2,1)S(1)} fusion(f32[64,32,64]{0,2,1:T(8,128)S(1)} %bitcast.59, f32[32,64,64]{2,1,0:T(8,128)S(1)} %reshape.64), kind=kOutput, calls=%fused_computation.4 | convolution fusion | flops 50462720 | bytes 1310720 | tf_op jit(solution)/shard_map/bmn,nbp->mbp/dot_general | solution.py:90
  59.5 0.0 copy-start
  59.5 0.3 copy.27
  59.8 17.6 %all_to_all.15 = bf16[64,16,128]{2,1,0:T(8,128)(2,1)S(1)} all-to-all(bf16[64,16,128]{2,1,0:T(8,128)(2,1)S(1)} %copy.27), channel_id=1, replica_groups=mesh['slab'=64,'obs'=8] {'slab'}, dimensions={0} | all-to-all | bytes 524288 | tf_op jit(solution)/shard_map/all_to_all | solution.py:92
  77.4 0.0 copy-done
  77.4 0.9 %convert_add_fusion = f32[64,16,128]{2,1,0:T(8,128)} fusion(f32[64,16,128]{2,1,0:T(8,128)S(1)} %bitcast.65, bf16[64,16,128]{2,1,0:T(8,128)(2,1)S(1)} %all_to_all.15), kind=kLoop, calls=%fused_computation.8 | loop fusion | flops 262144 | bytes 1310720 | tf_op jit(solution)/shard_map/add | solution.py:93
  (8 shorter events, 0.1 us)
Async XLA Ops:
  0.0 17.3 %copy-start.3 = (f32[1,32,8]{1,2,0:T(8,128)S(1)}, f32[1,32,8]{1,2,0:T(8,128)}, u32[]{:S(2)}) copy-start(f32[1,32,8]{1,2,0:T(8,128)} %param.15) | copy-start | bytes 3076
  0.0 17.4 %copy-start.1 = (s32[1,32,8]{1,2,0:T(8,128)S(1)}, s32[1,32,8]{1,2,0:T(8,128)}, u32[]{:S(2)}) copy-start(s32[1,32,8]{1,2,0:T(8,128)} %param.14) | copy-start | bytes 3076
  0.0 29.8 %copy-start.5 = (s32[1,1024]{1,0:T(1,128)S(1)}, s32[1,1024]{1,0:T(1,128)}, u32[]{:S(2)}) copy-start(s32[1,1024]{1,0:T(1,128)} %param.12) | copy-start | bytes 12292
  1.8 27.9 %all-to-all-start = ((bf16[64,16,128]{2,1,0:T(8,128)(2,1)}), bf16[64,16,128]{2,1,0:T(8,128)(2,1)S(1)}, u32[]{:S(2)}, u32[]{:S(2)}) async-start(bf16[64,16,128]{2,1,0:T(8,128)(2,1)} %convert.13), calls=%async_computation | async-start | bytes 524288 | tf_op jit(solution)/shard_map/all_to_all | solution.py:56
  29.8 1.6 %copy-start.2 = (f32[1,1024]{1,0:T(1,128)S(1)}, f32[1,1024]{1,0:T(1,128)}, u32[]{:S(2)}) copy-start(f32[1,1024]{1,0:T(1,128)} %param.11) | copy-start | bytes 12292
  29.8 1.6 %copy-start.4 = (bf16[64,1,1024]{2,0,1:T(8,128)(2,1)S(1)}, bf16[64,1,1024]{2,0,1:T(8,128)(2,1)}, u32[]{:S(2)}) copy-start(bf16[64,1,1024]{2,0,1:T(8,128)(2,1)} %param.9) | copy-start | bytes 393220
  29.8 1.6 %copy-start.6 = (f32[1,1024]{1,0:T(1,128)S(1)}, f32[1,1024]{1,0:T(1,128)}, u32[]{:S(2)}) copy-start(f32[1,1024]{1,0:T(1,128)} %param.10) | copy-start | bytes 12292
  32.7 24.8 %all-to-all-start.1 = ((bf16[8,16,2048]{2,1,0:T(8,128)(2,1)}), bf16[8,16,2048]{2,1,0:T(8,128)(2,1)S(1)}, u32[]{:S(2)}, u32[]{:S(2)}) async-start(bf16[8,16,2048]{2,1,0:T(8,128)(2,1)} %broadcast_in_dim.43), calls=%async_computation.1 | async-start | bytes 1048576 | tf_op jit(solution)/shard_map/all_to_all | solution.py:75
  59.5 17.9 %copy-start = (f32[1,131072]{1,0:T(1,128)S(1)}, f32[1,131072]{1,0:T(1,128)}, u32[]{:S(2)}) copy-start(f32[1,131072]{1,0:T(1,128)} %param.8) | copy-start | bytes 1572868

commit v13 on v11

--- a/solution.py
+++ b/solution.py
@@ -57,7 +57,6 @@
     tile_low = lax.optimization_barrier(tile.reshape(members, -1).astype(jnp.bfloat16))
     tile_work = tile_low.astype(jnp.float32)
     blocks = coupling_listing.shape[1]
-    deviation = tile_work - jnp.mean(tile_work, axis=0, keepdims=True)
 
     products = block_products(
         tile_low,
@@ -85,8 +84,14 @@
         localize_low, all_products, preferred_element_type=jnp.float32
     )
     ensemble = ensemble.reshape(blocks, members, members)
-    region_dev = deviation.reshape(members, blocks, -1)
-    increment = jnp.einsum("bmn,nbp->mbp", ensemble, region_dev, precision=lax.Precision.HIGH)
+    region_work = tile_low.reshape(members, blocks, -1)
+    ensemble_high = lax.optimization_barrier(ensemble.astype(jnp.bfloat16))
+    ensemble_low = (ensemble - ensemble_high.astype(jnp.float32)).astype(jnp.bfloat16)
+    increment = jnp.einsum(
+        "bmn,nbp->mbp", ensemble_high, region_work, preferred_element_type=jnp.float32
+    ) + jnp.einsum("bmn,nbp->mbp", ensemble_low, region_work, preferred_element_type=jnp.float32)
+    region_mean = jnp.mean(tile_work, axis=0).reshape(blocks, -1)
+    increment = increment - jnp.sum(ensemble, axis=2).T[:, :, None] * region_mean[None]
     increment_low = increment.reshape(members, -1, lanes).astype(jnp.bfloat16)
     back = lax.all_to_all(increment_low, "slab", split_axis=0, concat_axis=0, tiled=True)
     analysis = pieces + back.astype(jnp.float32)

time: 78.3 us -> 79 us (level)
  no operation moved by 1% of the time
where the time goes in v13:
time: 79 us; the launch traced here: 78.6 us
  waiting for transfers between devices  29.4 us (37%)
  starting transfers between devices  21.6 us (27%)
  blocking collectives  17.6 us (22%)
  other arithmetic  3.31 us (4%)
  matrix products  2.99 us (4%)
  local copies, waits for them, and re-layouts  2.85 us (4%)
  between operations  0.89 us (1%)
    all_to_all x1, blocking collectives, local(): lax.all_to_all(increment_low, 'slab', split_axis=0, concat_axis=0, tiled=...  17.6 us
    all_to_all x1, waiting for transfers between devices, local(): lax.all_to_all(copies, 'obs', split_axis=0, concat_axis=0, tiled=True)  17 us
    all_to_all x1, starting transfers between devices, local(): lax.all_to_all(pieces, 'slab', split_axis=0, concat_axis=0, tiled=True)  14.8 us
    all_to_all x1, waiting for transfers between devices, local(): lax.all_to_all(pieces, 'slab', split_axis=0, concat_axis=0, tiled=True)  12.4 us
    all_to_all x1, starting transfers between devices, local(): lax.all_to_all(copies, 'obs', split_axis=0, concat_axis=0, tiled=True)  6.82 us
    unnamed x1, other arithmetic  1.79 us
  transfers between devices with their start and end apart: 2, of which 2 were waited for; matrix products, arithmetic and copies ran while one was open for 1% of the time, Pallas kernels for 0%

profile of v13, /device:TPU:1, one launch (start us, length us, event | category | flops | bytes accessed | tf_op | source)
XLA Modules:
  0.0 78.6 jit_solution(7092559434281457556)
XLA Ops:
  0.0 0.0 copy-start.5
  0.0 1.8 %convert.13 = bf16[64,16,128]{2,1,0:T(8,128)(2,1)} convert(f32[64,16,128]{2,1,0:T(8,128)} %bitcast.67) | non-fusion elementwise | flops 131072 | bytes 786432
  1.8 14.8 %all-to-all-start = ((bf16[64,16,128]{2,1,0:T(8,128)(2,1)}), bf16[64,16,128]{2,1,0:T(8,128)(2,1)S(1)}, u32[]{:S(2)}, u32[]{:S(2)}) async-start(bf16[64,16,128]{2,1,0:T(8,128)(2,1)} %convert.13), calls=%async_computation | async-start | bytes 524288 | tf_op jit(solution)/shard_map/all_to_all | solution.py:56
  17.3 12.4 %all-to-all-done = bf16[64,16,128]{2,1,0:T(8,128)(2,1)S(1)} async-done(((bf16[64,16,128]{2,1,0:T(8,128)(2,1)}), bf16[64,16,128]{2,1,0:T(8,128)(2,1)S(1)}, u32[]{:S(2)}, u32[]{:S(2)}) %all-to-all-start) | async-done | bytes 262176 | tf_op jit(solution)/shard_map/all_to_all | solution.py:56
  29.7 0.1 copy.43
  29.8 0.0 copy-done.5
  29.8 0.0 copy-start.1
  29.8 0.0 copy-start.4
  29.8 0.0 copy-start.6
  29.8 1.5 %fusion.23 = (f32[1024]{0:T(1024)S(1)}, f32[1024,64]{0,1:T(8,128)S(1)}) fusion(bf16[64,2048]{1,0:T(8,128)(2,1)S(1)} %bitcast.64, s32[1024]{0:T(1024)S(1)} %bitcast.74), kind=kOutput, calls=%fused_computation.42 | convolution fusion | flops 270597120 | bytes 532480 | tf_op jit(solution)/shard_map/dot_general | solution.py:26
  31.3 0.1 multiply_reduce_fusion
  31.4 0.0 copy-done.1
  31.4 0.0 copy-done.4
  31.4 0.0 copy-done.6
  31.4 0.2 convolution_convert_fusion
  31.6 0.0 copy-start.3
  31.6 0.0 copy-start.2
  31.7 0.2 broadcast_in_dim.42
  31.8 0.8 %broadcast_in_dim.43 = bf16[8,8,4096]{2,1,0:T(8,128)(2,1)} broadcast(bf16[8,4096]{1,0:T(8,128)(2,1)S(1)} %broadcast_in_dim.42), dimensions={1,2} | broadcast | bytes 589824 | tf_op jit(solution)/shard_map/broadcast_in_dim | solution.py:72
  32.7 6.8 %all-to-all-start.1 = ((bf16[8,8,4096]{2,1,0:T(8,128)(2,1)}), bf16[8,8,4096]{2,1,0:T(8,128)(2,1)S(1)}, u32[]{:S(2)}, u32[]{:S(2)}) async-start(bf16[8,8,4096]{2,1,0:T(8,128)(2,1)} %broadcast_in_dim.43), calls=%async_computation.1 | async-start | bytes 1048576 | tf_op jit(solution)/shard_map/all_to_all | solution.py:73
  39.5 0.0 copy-done.3
  39.5 0.1 copy.21
  39.6 0.0 copy-done.2
  39.6 0.1 copy.20
  39.7 0.1 select_reduce_fusion
  39.8 0.5 reshape.68
  40.3 0.1 convert_reduce_fusion
  40.4 0.1 div.53
  40.5 17.0 %all-to-all-done.1 = bf16[8,8,4096]{2,1,0:T(8,128)(2,1)S(1)} async-done(((bf16[8,8,4096]{2,1,0:T(8,128)(2,1)}), bf16[8,8,4096]{2,1,0:T(8,128)(2,1)S(1)}, u32[]{:S(2)}, u32[]{:S(2)}) %all-to-all-start.1) | async-done | bytes 524320 | tf_op jit(solution)/shard_map/all_to_all | solution.py:73
  57.4 0.2 fusion.6
  57.7 0.2 convolution_add_fusion
  57.9 0.4 reshape.67
  58.3 0.4 fusion.22
  58.7 0.3 fusion.9
  59.0 0.5 fusion.4
  59.6 0.0 copy-start
  59.6 0.3 copy.26
  60.0 0.2 convert_element_type.67
  60.2 17.6 %all_to_all.15 = bf16[64,16,128]{2,1,0:T(8,128)(2,1)S(1)} all-to-all(bf16[64,16,128]{2,1,0:T(8,128)(2,1)S(1)} %convert_element_type.67), channel_id=1, replica_groups=mesh['slab'=64,'obs'=8] {'slab'}, dimensions={0} | all-to-all | bytes 524288 | tf_op jit(solution)/shard_map/all_to_all | solution.py:96
  77.8 0.0 copy-done
  77.8 0.8 %convert_add_fusion = f32[64,16,128]{2,1,0:T(8,128)} fusion(f32[64,16,128]{2,1,0:T(8,128)S(1)} %bitcast.68, bf16[64,16,128]{2,1,0:T(8,128)(2,1)S(1)} %all_to_all.15), kind=kLoop, calls=%fused_computation.13 | loop fusion | flops 262144 | bytes 1310720 | tf_op jit(solution)/shard_map/add | solution.py:97
  (7 shorter events, 0.0 us)
Async XLA Ops:
  0.0 29.8 %copy-start.5 = (s32[1,1024]{1,0:T(1,128)S(1)}, s32[1,1024]{1,0:T(1,128)}, u32[]{:S(2)}) copy-start(s32[1,1024]{1,0:T(1,128)} %param.12) | copy-start | bytes 12292
  1.8 27.9 %all-to-all-start = ((bf16[64,16,128]{2,1,0:T(8,128)(2,1)}), bf16[64,16,128]{2,1,0:T(8,128)(2,1)S(1)}, u32[]{:S(2)}, u32[]{:S(2)}) async-start(bf16[64,16,128]{2,1,0:T(8,128)(2,1)} %convert.13), calls=%async_computation | async-start | bytes 524288 | tf_op jit(solution)/shard_map/all_to_all | solution.py:56
  29.8 1.6 %copy-start.1 = (f32[1,1024]{1,0:T(1,128)S(1)}, f32[1,1024]{1,0:T(1,128)}, u32[]{:S(2)}) copy-start(f32[1,1024]{1,0:T(1,128)} %param.11) | copy-start | bytes 12292
  29.8 1.6 %copy-start.4 = (bf16[64,1,1024]{2,0,1:T(8,128)(2,1)S(1)}, bf16[64,1,1024]{2,0,1:T(8,128)(2,1)}, u32[]{:S(2)}) copy-start(bf16[64,1,1024]{2,0,1:T(8,128)(2,1)} %param.9) | copy-start | bytes 393220
  29.8 1.6 %copy-start.6 = (f32[1,1024]{1,0:T(1,128)S(1)}, f32[1,1024]{1,0:T(1,128)}, u32[]{:S(2)}) copy-start(f32[1,1024]{1,0:T(1,128)} %param.10) | copy-start | bytes 12292
  31.6 7.9 %copy-start.3 = (f32[1,32,8]{1,2,0:T(8,128)S(1)}, f32[1,32,8]{1,2,0:T(8,128)}, u32[]{:S(2)}) copy-start(f32[1,32,8]{1,2,0:T(8,128)} %param.15) | copy-start | bytes 3076
  31.6 7.9 %copy-start.2 = (s32[1,32,8]{1,2,0:T(8,128)S(1)}, s32[1,32,8]{1,2,0:T(8,128)}, u32[]{:S(2)}) copy-start(s32[1,32,8]{1,2,0:T(8,128)} %param.14) | copy-start | bytes 3076
  32.7 24.8 %all-to-all-start.1 = ((bf16[8,8,4096]{2,1,0:T(8,128)(2,1)}), bf16[8,8,4096]{2,1,0:T(8,128)(2,1)S(1)}, u32[]{:S(2)}, u32[]{:S(2)}) async-start(bf16[8,8,4096]{2,1,0:T(8,128)(2,1)} %broadcast_in_dim.43), calls=%async_computation.1 | async-start | bytes 1048576 | tf_op jit(solution)/shard_map/all_to_all | solution.py:73
  59.6 18.2 %copy-start = (f32[1,131072]{1,0:T(1,128)S(1)}, f32[1,131072]{1,0:T(1,128)}, u32[]{:S(2)}) copy-start(f32[1,131072]{1,0:T(1,128)} %param.8) | copy-start | bytes 1572868

commit v14 on v11

--- a/solution.py
+++ b/solution.py
@@ -22,8 +22,8 @@
     positions = measurement_grid_location[0]
     obs_count = positions.shape[0]
     points = tile_work.shape[1]
-    pick = (jnp.arange(points, dtype=jnp.int32)[:, None] == positions[None, :]).astype(jnp.bfloat16)
-    prior_value = jnp.dot(tile_low, pick, preferred_element_type=jnp.float32)
+    pick = (positions[:, None] == jnp.arange(points, dtype=jnp.int32)[None, :]).astype(jnp.bfloat16)
+    prior_value = jnp.einsum("kq,mq->mk", pick, tile_low, preferred_element_type=jnp.float32)
     prior_shift = prior_value - jnp.mean(prior_value, axis=0, keepdims=True)
     spread = jnp.sum(prior_shift * prior_shift, axis=0, keepdims=True) / (members - 1)
     usable = jnp.arange(obs_count, dtype=jnp.int32)[None, :] < active_tallies[0, 0]

time: 78.3 us -> 78.7 us (level)
  no operation moved by 1% of the time
where the time goes in v14:
time: 78.7 us; the launch traced here: 78.4 us
  waiting for transfers between devices  29.6 us (38%)
  starting transfers between devices  21.6 us (27%)
  blocking collectives  17.6 us (22%)
  matrix products  3.46 us (4%)
  other arithmetic  3 us (4%)
  local copies, waits for them, and re-layouts  2.29 us (3%)
  between operations  0.87 us (1%)
    all_to_all x1, blocking collectives, local(): lax.all_to_all(increment_low, 'slab', split_axis=0, concat_axis=0, tiled=...  17.6 us
    all_to_all x1, waiting for transfers between devices, local(): lax.all_to_all(copies, 'obs', split_axis=0, concat_axis=0, tiled=True)  17.3 us
    all_to_all x1, starting transfers between devices, local(): lax.all_to_all(pieces, 'slab', split_axis=0, concat_axis=0, tiled=True)  14.8 us
    all_to_all x1, waiting for transfers between devices, local(): lax.all_to_all(pieces, 'slab', split_axis=0, concat_axis=0, tiled=True)  12.2 us
    all_to_all x1, starting transfers between devices, local(): lax.all_to_all(copies, 'obs', split_axis=0, concat_axis=0, tiled=True)  6.82 us
    dot_general x1, matrix products, block_products(): jnp.einsum('kq,mq->mk', pick, tile_low, preferred_element_type=jnp.float32)  1.87 us
    unnamed x1, other arithmetic  1.82 us
  transfers between devices with their start and end apart: 2, of which 2 were waited for; matrix products, arithmetic and copies ran while one was open for 1% of the time, Pallas kernels for 0%

profile of v14, /device:TPU:1, one launch (start us, length us, event | category | flops | bytes accessed | tf_op | source)
XLA Modules:
  0.0 78.4 jit_solution(8185269128919612201)
XLA Ops:
  0.0 0.0 copy-start.3
  0.0 0.0 copy-start.1
  0.0 0.0 copy-start.5
  0.0 1.8 %convert.13 = bf16[64,16,128]{2,1,0:T(8,128)(2,1)} convert(f32[64,16,128]{2,1,0:T(8,128)} %bitcast.67) | non-fusion elementwise | flops 131072 | bytes 786432
  1.8 14.8 %all-to-all-start = ((bf16[64,16,128]{2,1,0:T(8,128)(2,1)}), bf16[64,16,128]{2,1,0:T(8,128)(2,1)S(1)}, u32[]{:S(2)}, u32[]{:S(2)}) async-start(bf16[64,16,128]{2,1,0:T(8,128)(2,1)} %convert.13), calls=%async_computation | async-start | bytes 524288 | tf_op jit(solution)/shard_map/all_to_all | solution.py:56
  17.3 0.0 copy-done.3
  17.3 0.1 copy.24
  17.4 0.0 copy-done.1
  17.4 0.1 copy.23
  17.5 12.2 %all-to-all-done = bf16[64,16,128]{2,1,0:T(8,128)(2,1)S(1)} async-done(((bf16[64,16,128]{2,1,0:T(8,128)(2,1)}), bf16[64,16,128]{2,1,0:T(8,128)(2,1)S(1)}, u32[]{:S(2)}, u32[]{:S(2)}) %all-to-all-start) | async-done | bytes 262176 | tf_op jit(solution)/shard_map/all_to_all | solution.py:56
  29.7 0.1 copy.40
  29.8 0.0 copy-done.5
  29.8 0.0 copy-start.2
  29.8 0.0 copy-start.4
  29.8 0.0 copy-start.6
  29.9 1.9 %fusion.16 = (f32[1024]{0:T(1024)S(1)}, f32[1024,64]{0,1:T(8,128)S(1)}) fusion(bf16[64,2048]{1,0:T(8,128)(2,1)S(1)} %bitcast.63, s32[1024]{0:T(1024)S(1)} %bitcast.73), kind=kOutput, calls=%fused_computation.35 | convolution fusion | flops 270597120 | bytes 532480 | tf_op jit(solution)/shard_map/kq,mq->mk/dot_general | solution.py:26
  31.7 0.1 multiply_reduce_fusion
  31.8 0.0 copy-done.2
  31.8 0.0 copy-done.4
  31.8 0.0 copy-done.6
  31.9 0.2 convolution_convert_fusion.1
  32.1 0.2 broadcast_in_dim.42
  32.3 0.8 %broadcast_in_dim.43 = bf16[8,8,4096]{2,1,0:T(8,128)(2,1)} broadcast(bf16[8,4096]{1,0:T(8,128)(2,1)S(1)} %broadcast_in_dim.42), dimensions={1,2} | broadcast | bytes 589824 | tf_op jit(solution)/shard_map/broadcast_in_dim | solution.py:73
  33.1 6.8 %all-to-all-start.1 = ((bf16[8,8,4096]{2,1,0:T(8,128)(2,1)}), bf16[8,8,4096]{2,1,0:T(8,128)(2,1)S(1)}, u32[]{:S(2)}, u32[]{:S(2)}) async-start(bf16[8,8,4096]{2,1,0:T(8,128)(2,1)} %broadcast_in_dim.43), calls=%async_computation.1 | async-start | bytes 1048576 | tf_op jit(solution)/shard_map/all_to_all | solution.py:74
  39.9 0.1 select_reduce_fusion
  40.1 0.1 convert_reduce_fusion
  40.2 0.3 copy.22
  40.5 17.3 %all-to-all-done.1 = bf16[8,8,4096]{2,1,0:T(8,128)(2,1)S(1)} async-done(((bf16[8,8,4096]{2,1,0:T(8,128)(2,1)}), bf16[8,8,4096]{2,1,0:T(8,128)(2,1)S(1)}, u32[]{:S(2)}, u32[]{:S(2)}) %all-to-all-start.1) | async-done | bytes 524320 | tf_op jit(solution)/shard_map/all_to_all | solution.py:74
  57.9 0.2 fusion.3
  58.1 0.2 convolution_add_fusion
  58.3 0.4 reshape.65
  58.7 1.0 %convolution_convert_fusion = bf16[32,64,64]{2,1,0:T(8,128)(2,1)S(1)} fusion(f32[64,32,64]{0,2,1:T(8,128)S(1)} %bitcast.62, f32[32,64,64]{2,1,0:T(8,128)S(1)} %reshape.65), kind=kOutput, calls=%fused_computation.4 | convolution fusion | flops 50462720 | bytes 1310720 | tf_op jit(solution)/shard_map/bmn,nbp->mbp/dot_general | solution.py:89
  59.7 0.0 copy-start
  59.7 0.3 copy.27
  60.0 17.6 %all_to_all.15 = bf16[64,16,128]{2,1,0:T(8,128)(2,1)S(1)} all-to-all(bf16[64,16,128]{2,1,0:T(8,128)(2,1)S(1)} %copy.27), channel_id=1, replica_groups=mesh['slab'=64,'obs'=8] {'slab'}, dimensions={0} | all-to-all | bytes 524288 | tf_op jit(solution)/shard_map/all_to_all | solution.py:91
  77.6 0.0 copy-done
  77.6 0.9 %convert_add_fusion = f32[64,16,128]{2,1,0:T(8,128)} fusion(f32[64,16,128]{2,1,0:T(8,128)S(1)} %bitcast.68, bf16[64,16,128]{2,1,0:T(8,128)(2,1)S(1)} %all_to_all.15), kind=kLoop, calls=%fused_computation.11 | loop fusion | flops 262144 | bytes 1310720 | tf_op jit(solution)/shard_map/add | solution.py:92
  (8 shorter events, 0.1 us)
Async XLA Ops:
  0.0 17.3 %copy-start.3 = (f32[1,32,8]{1,2,0:T(8,128)S(1)}, f32[1,32,8]{1,2,0:T(8,128)}, u32[]{:S(2)}) copy-start(f32[1,32,8]{1,2,0:T(8,128)} %param.15) | copy-start | bytes 3076
  0.0 17.4 %copy-start.1 = (s32[1,32,8]{1,2,0:T(8,128)S(1)}, s32[1,32,8]{1,2,0:T(8,128)}, u32[]{:S(2)}) copy-start(s32[1,32,8]{1,2,0:T(8,128)} %param.14) | copy-start | bytes 3076
  0.0 29.8 %copy-start.5 = (s32[1,1024]{1,0:T(1,128)S(1)}, s32[1,1024]{1,0:T(1,128)}, u32[]{:S(2)}) copy-start(s32[1,1024]{1,0:T(1,128)} %param.12) | copy-start | bytes 12292
  1.8 27.9 %all-to-all-start = ((bf16[64,16,128]{2,1,0:T(8,128)(2,1)}), bf16[64,16,128]{2,1,0:T(8,128)(2,1)S(1)}, u32[]{:S(2)}, u32[]{:S(2)}) async-start(bf16[64,16,128]{2,1,0:T(8,128)(2,1)} %convert.13), calls=%async_computation | async-start | bytes 524288 | tf_op jit(solution)/shard_map/all_to_all | solution.py:56
  29.8 2.0 %copy-start.2 = (f32[1,1024]{1,0:T(1,128)S(1)}, f32[1,1024]{1,0:T(1,128)}, u32[]{:S(2)}) copy-start(f32[1,1024]{1,0:T(1,128)} %param.11) | copy-start | bytes 12292
  29.8 2.0 %copy-start.4 = (bf16[64,1,1024]{2,0,1:T(8,128)(2,1)S(1)}, bf16[64,1,1024]{2,0,1:T(8,128)(2,1)}, u32[]{:S(2)}) copy-start(bf16[64,1,1024]{2,0,1:T(8,128)(2,1)} %param.9) | copy-start | bytes 393220
  29.8 2.0 %copy-start.6 = (f32[1,1024]{1,0:T(1,128)S(1)}, f32[1,1024]{1,0:T(1,128)}, u32[]{:S(2)}) copy-start(f32[1,1024]{1,0:T(1,128)} %param.10) | copy-start | bytes 12292
  33.1 24.8 %all-to-all-start.1 = ((bf16[8,8,4096]{2,1,0:T(8,128)(2,1)}), bf16[8,8,4096]{2,1,0:T(8,128)(2,1)S(1)}, u32[]{:S(2)}, u32[]{:S(2)}) async-start(bf16[8,8,4096]{2,1,0:T(8,128)(2,1)} %broadcast_in_dim.43), calls=%async_computation.1 | async-start | bytes 1048576 | tf_op jit(solution)/shard_map/all_to_all | solution.py:74
  59.7 17.9 %copy-start = (f32[1,131072]{1,0:T(1,128)S(1)}, f32[1,131072]{1,0:T(1,128)}, u32[]{:S(2)}) copy-start(f32[1,131072]{1,0:T(1,128)} %param.8) | copy-start | bytes 1572868
